TPU v7x, 512 devices: a whole 4x8x8 slice. The times are simulated.
512 devices in a mesh: shard: 128 (over y, z, core), tensor: 4 (over x).
Axes of the slice: x: 4, y: 8, z: 8, core: 2. Of those that a mesh axis runs over, the one named last changes fastest.
Arguments:
- big_grad: bfloat16 [32, 1280, 768], P(None, 'shard', 'tensor')
- big_weight: bfloat16 [32, 1280, 768], P(None, 'shard', 'tensor'), may hold values from -0.017944336 to 0.017944336
- big_moment: float32 [128, 768, 1280], P('shard', 'tensor'), may hold values from -6 to 6
- small_grad: bfloat16 [32, 1280, 192], P(None, 'shard')
- small_weight: bfloat16 [32, 1280, 192], P(None, 'shard'), may hold values from -0.15625 to 0.15625
- small_moment: float32 [128, 192, 1280], P('shard'), may hold values from -6 to 6
- owners: int32 [2, 32], replicated, may hold values from 0 to 127, as said below
- vec_parts: float32 [128, 43008], P('shard'), may hold values from -0.6 to 0.6
- vec_param: float32 [43008], P('shard'), may hold values from 0.5 to 1.5
- vec_first: float32 [43008], P('shard'), may hold values from -0.6 to 0.6
- vec_second: float32 [43008], P('shard'), may hold values from 0.01 to 1
Outputs:
- big_weight_new: bfloat16 [32, 1280, 768], P(None, 'shard', 'tensor')
- big_moment_new: float32 [128, 768, 1280], P('shard', 'tensor')
- small_weight_new: bfloat16 [32, 1280, 192], P(None, 'shard')
- small_moment_new: float32 [128, 192, 1280], P('shard')
- vec_param_new: float32 [43008], P('shard')
- vec_first_new: float32 [43008], P('shard')
- vec_second_new: float32 [43008], P('shard')
Inputs may be any that keep to these rules, and one draw needn't show every extreme that they name: `owners`: no shard index appears twice in the whole list (over both rows); each aligned group of four shard indices holds exactly one owner of each row; the first and the last shard index own a matrix.
All inputs are finite; a program needn't handle non-finite values.
Results may differ from a plain program's by a relative error of at most 0.0068.
Values may be sent and summed in bfloat16 or wider, within the bound.
No kernel may reach another device: no remote copies, remote signals or barrier semaphores. Data moves between devices by JAX's collectives and lax.ppermute only.
A program may use at most 64 MiB of HBM per device.

v0:
```python
import math

import jax
import jax.numpy as jnp
from jax import lax
from jax.sharding import PartitionSpec as P

D = 1280
ITERS = 2


newton_linear = 3.4445
newton_cubic = -4.775
newton_quintic = 2.0315
momentum_rate = 0.95
muon_rate = 0.05
weight_decay = 0.1
norm_epsilon = 1e-07
adam_rate = 0.004
first_decay = 0.9
second_decay = 0.95
adam_epsilon = 1e-08
first_correct = 0.99997343860111
second_correct = 0.99407947077967


def owner_table(owner_list, count):
    devices = lax.broadcasted_iota(jnp.int32, (count, owner_list.shape[0]), 0)
    return (devices == owner_list[None, :]).astype(jnp.bfloat16)


def route_rows(owner_map, pieces):
    flattened = pieces.reshape(pieces.shape[0], -1)
    routed = jnp.dot(owner_map, flattened, preferred_element_type=jnp.float32)
    return routed.astype(jnp.bfloat16).reshape((owner_map.shape[0],) + pieces.shape[1:])


def collect(owner_map, arrived):
    flattened = arrived.reshape(arrived.shape[0], -1)
    picked = lax.dot_general(
        owner_map, flattened, (((0,), (0,)), ((), ())), preferred_element_type=jnp.float32
    )
    return picked.astype(jnp.bfloat16).reshape((owner_map.shape[1],) + arrived.shape[1:])


def advance(arrived, moment, is_owner):
    gradient = arrived.T.astype(jnp.float32)
    renewed = momentum_rate * moment + gradient
    retained = jnp.where(is_owner, renewed, moment)
    blended = jnp.where(is_owner, gradient + momentum_rate * renewed, 0.0).astype(jnp.bfloat16).T
    return (retained, blended)


def normalized(field):
    values = field.astype(jnp.float32)
    squares = jnp.sum(values * values)
    return (values / (jnp.sqrt(squares) + norm_epsilon)).astype(jnp.bfloat16)


def gram_block(left_part, right_part):
    product = lax.dot_general(
        left_part, right_part, (((0,), (0,)), ((), ())), preferred_element_type=jnp.float32
    )
    return product.astype(jnp.bfloat16)


def poly_block(gram_part, gram_full):
    square = jnp.dot(gram_part, gram_full, preferred_element_type=jnp.float32)
    return (newton_cubic * gram_part.astype(jnp.float32) + newton_quintic * square).astype(
        jnp.bfloat16
    )


def newton_step(column_part, full_iterate, polynomial):
    product = lax.dot_general(
        full_iterate, polynomial, (((1,), (1,)), ((), ())), preferred_element_type=jnp.float32
    )
    return (newton_linear * column_part.astype(jnp.float32) + product).astype(jnp.bfloat16)


def small_newton(field):
    iterate = normalized(field)
    for iteration in range(ITERS):
        gram_full = gram_block(iterate, iterate)
        iterate = newton_step(iterate, iterate, poly_block(gram_full, gram_full))
    return iterate


def apply_update(weight, update):
    scale = 0.2 * math.sqrt(D)
    values = weight.astype(jnp.float32)
    return (
        values - muon_rate * (scale * update.astype(jnp.float32) + weight_decay * values)
    ).astype(jnp.bfloat16)


def gather_columns(column_part):
    return lax.all_gather(column_part, "tensor", axis=1, tiled=True)


def gather_gram(gram_part):
    return lax.all_gather(gram_part, "tensor", axis=0, tiled=True)


def per_device(
    big_grad,
    big_weight,
    big_moment,
    small_grad,
    small_weight,
    small_moment,
    owners,
    vec_parts,
    vec_param,
    vec_first,
    vec_second,
):
    shards = lax.axis_size("shard")
    shard_place = lax.axis_index("shard")
    column = lax.axis_index("tensor")
    block_width = big_grad.shape[2]
    rows_dev = big_grad.shape[1]
    matrices = big_grad.shape[0]
    joint_map = owner_table(jnp.concatenate([owners[0], owners[1]]), shards)
    joint_pieces = jnp.concatenate([big_grad, small_grad], axis=0)
    arrived = lax.all_to_all(
        route_rows(joint_map, joint_pieces), "shard", split_axis=0, concat_axis=1, tiled=True
    )[0]
    big_owner = jnp.any(owners[0] == shard_place)
    small_owner = jnp.any(owners[1] == shard_place)
    big_retained, big_blended = advance(arrived, big_moment[0], big_owner)
    small_retained, small_blended = advance(arrived, small_moment[0], small_owner)
    small_result = small_newton(small_blended)
    full_iterate = normalized(gather_columns(big_blended))
    for iteration in range(ITERS):
        owned_part = lax.dynamic_slice_in_dim(full_iterate, column * block_width, block_width, 1)
        gram_full = gather_gram(gram_block(owned_part, full_iterate))
        full_iterate = newton_step(full_iterate, full_iterate, poly_block(gram_full, gram_full))
    big_result = lax.dynamic_slice_in_dim(full_iterate, column * block_width, block_width, 1)
    own_result = jnp.where(big_owner, big_result, small_result)
    returned = lax.all_to_all(
        own_result.reshape(shards, rows_dev, block_width),
        "shard",
        split_axis=0,
        concat_axis=0,
        tiled=True,
    )
    picked = collect(joint_map, returned)
    big_weight_new = apply_update(big_weight, picked[:matrices])
    small_weight_new = apply_update(small_weight, picked[matrices:])
    grad_share = lax.psum_scatter(vec_parts[0], "shard", scatter_dimension=0, tiled=True)
    first_new = first_decay * vec_first + (1.0 - first_decay) * grad_share
    second_new = second_decay * vec_second + (1.0 - second_decay) * grad_share * grad_share
    param_new = vec_param - adam_rate * (first_new / first_correct) / (
        jnp.sqrt(second_new / second_correct) + adam_epsilon
    )
    return (
        big_weight_new,
        big_retained[None],
        small_weight_new,
        small_retained[None],
        param_new,
        first_new,
        second_new,
    )


def solution(mesh):
    return jax.shard_map(
        per_device,
        mesh=mesh,
        in_specs=(
            P(None, "shard", "tensor"),
            P(None, "shard", "tensor"),
            P("shard", "tensor", None),
            P(None, "shard", None),
            P(None, "shard", None),
            P("shard", None, None),
            P(),
            P("shard", None),
            P("shard"),
            P("shard"),
            P("shard"),
        ),
        out_specs=(
            P(None, "shard", "tensor"),
            P("shard", "tensor", None),
            P(None, "shard", None),
            P("shard", None, None),
            P("shard"),
            P("shard"),
            P("shard"),
        ),
        check_vma=False,
    )
```

profile of v0, /device:TPU:1, one launch (start us, length us, event | category | flops | bytes accessed | tf_op | source)
XLA Modules:
  0.0 395.7 jit_solution(8860446382771876976)
XLA Ops:
  8.0 0.8 slice_bitcast_fusion.1
  8.8 1.0 pad_maximum_fusion
  11.0 1.3 copy.34
  12.4 1.6 reshape.48
  13.9 18.4 %all-to-all-start = ((bf16[128,2,960]{2,1,0:T(2,128)(2,1)}), bf16[128,2,960]{2,1,0:T(2,128)(2,1)S(1)}, u32[]{:S(2)}, u32[]{:S(2)}) async-start(bf16[128,2,960]{2,1,0:T(2,128)(2,1)} %reshape.48), calls=%async_computation | async-start | bytes 1048576 | tf_op jit(solution)/shard_map/all_to_all | solution.py:126
  32.4 0.6 compare_reduce_fusion.1
  33.1 18.7 %all-to-all-done = bf16[128,2,960]{2,1,0:T(2,128)(2,1)S(1)} async-done(((bf16[128,2,960]{2,1,0:T(2,128)(2,1)}), bf16[128,2,960]{2,1,0:T(2,128)(2,1)S(1)}, u32[]{:S(2)}, u32[]{:S(2)}) %all-to-all-start) | async-done | bytes 491552 | tf_op jit(solution)/shard_map/all_to_all | solution.py:126
  51.8 0.8 reshape.49
  52.9 0.4 copy.35
  53.3 0.8 copy-done.2
  54.1 4.9 %fusion.15 = (f32[1,192,1280]{2,1,0:T(8,128)}, bf16[1280,192]{0,1:T(8,128)(2,1)}, f32[1,192,1280]{2,1,0:T(8,128)}, f32[]{:T(128)}, bf16[192,1280]{1,0:T(8,128)(2,1)S(1)}) fusion(f32[1,192,1280]{2,1,0:T(8,128)S(1)} %copy-done.2, f32[1280,192]{0,1:T(8,128)S(1)} %copy.35, pred[]{:T(512)} %get-tuple-element.21, f32[1,192,1280]{2,1,0:T(8,128)} %param.16, ...), kind=kLoop, calls=%fused_computation.37 | loop fusion | flops 4177919 | bytes 5898246 | tf_op jit(solution)/shard_map/broadcast_in_dim | solution.py:159
  59.0 28.6 %all-gather.4.cloned.1.call-done = bf16[1280,768]{0,1:T(8,128)(2,1)} async-done(((bf16[1280,192]{0,1:T(8,128)(2,1)}), bf16[1280,768]{0,1:T(8,128)(2,1)}) %all-gather.4.cloned.1.call-update) | async-done | bytes 1966096 | tf_op jit(solution)/shard_map/all_gather | solution.py:98
  87.6 3.3 fusion
  92.0 1.3 copy-done.1
  93.3 1.5 convolution_convert_fusion.3
  95.1 27.7 %all-gather.6.cloned.1.call-done = bf16[768,768]{1,0:T(8,128)(2,1)} async-done(((bf16[192,768]{1,0:T(8,128)(2,1)}), bf16[768,768]{1,0:T(8,128)(2,1)}) %all-gather.6.cloned.1.call-update) | async-done | bytes 1179664 | tf_op jit(solution)/shard_map/all_gather | solution.py:102
  122.8 6.0 %add_convert_fusion = bf16[1280,768]{0,1:T(8,128)(2,1)S(1)} fusion(bf16[1280,768]{0,1:T(8,128)(2,1)} %copy-done.1, bf16[768,768]{1,0:T(8,128)(2,1)} %all-gather.6.cloned.1.call-done), kind=kOutput, calls=%fused_computation.4 | convolution fusion | flops 2422800384 | bytes 5111808 | tf_op jit(solution)/shard_map/dot_general | solution.py:75
  128.8 1.5 convolution_convert_fusion.2
  131.4 0.5 fusion.2
  132.2 28.7 %all-gather.8.cloned.1.call-done = bf16[768,768]{1,0:T(8,128)(2,1)} async-done(((bf16[192,768]{1,0:T(8,128)(2,1)}), bf16[768,768]{1,0:T(8,128)(2,1)}) %all-gather.8.cloned.1.call-update) | async-done | bytes 1179664 | tf_op jit(solution)/shard_map/all_gather | solution.py:102
  160.8 7.5 %fusion.20 = f32[1280,768]{0,1:T(8,128)} fusion(bf16[1280,768]{0,1:T(8,128)(2,1)} %copy-done.9, bf16[768,768]{1,0:T(8,128)(2,1)} %all-gather.8.cloned.1.call-done), kind=kOutput, calls=%fused_computation.44 | convolution fusion | flops 2418868224 | bytes 7077888 | tf_op jit(solution)/shard_map/dot_general | solution.py:75
  168.3 2.4 fusion.4
  171.3 1.6 reshape.50
  172.9 16.4 %all-to-all-start.1 = ((bf16[128,2,960]{2,1,0:T(2,128)(2,1)}), bf16[128,2,960]{2,1,0:T(2,128)(2,1)S(1)}, u32[]{:S(2)}, u32[]{:S(2)}) async-start(bf16[128,2,960]{2,1,0:T(2,128)(2,1)} %reshape.50), calls=%async_computation.1 | async-start | bytes 1048576 | tf_op jit(solution)/shard_map/all_to_all | solution.py:141
  189.4 0.5 all-reduce.3.cloned.1.call-update
  189.9 1.3 dynamic-slice
  191.8 191.3 %all-reduce.3.cloned.1.call-done = f32[43008]{0:T(1024)} async-done(((f32[43008]{0:T(1024)}), f32[43008]{0:T(1024)}) %all-reduce.3.cloned.1.call-update) | async-done | bytes 172048
  383.2 1.4 divide_subtract_fusion
  384.5 0.8 reshape.51
  385.3 0.7 copy.37
  386.8 0.7 copy.39
  387.9 0.7 copy.40
  (43 shorter events, 4.5 us)
Async XLA Ops:
  11.0 21.4 %copy-start.5 = (s32[2,32]{1,0:T(2,128)S(1)}, s32[2,32]{1,0:T(2,128)}, u32[]{:S(2)}) copy-start(s32[2,32]{1,0:T(2,128)} %param.17) | copy-start | bytes 772
  13.9 37.8 %all-to-all-start = ((bf16[128,2,960]{2,1,0:T(2,128)(2,1)}), bf16[128,2,960]{2,1,0:T(2,128)(2,1)S(1)}, u32[]{:S(2)}, u32[]{:S(2)}) async-start(bf16[128,2,960]{2,1,0:T(2,128)(2,1)} %reshape.48), calls=%async_computation | async-start | bytes 1048576 | tf_op jit(solution)/shard_map/all_to_all | solution.py:126
  32.4 55.2 %all-gather.4.cloned.1.call-start = ((), (), s32[]{:S(2)}) async-start(), calls=%async_computation.2 | async-start | bytes 2457600 | tf_op jit(solution)/shard_map/all_gather | solution.py:98
  52.9 1.2 copy-start.2
  59.0 63.8 %all-gather.6.cloned.1.call-start = ((), (), s32[]{:S(2)}) async-start(), calls=%async_computation.3 | async-start | bytes 1474560 | tf_op jit(solution)/shard_map/all_gather | solution.py:102
  87.6 4.0 %copy-start = (bf16[1280,768]{0,1:T(8,128)(2,1)S(1)}, bf16[1280,768]{0,1:T(8,128)(2,1)}, u32[]{:S(2)}) copy-start(bf16[1280,768]{0,1:T(8,128)(2,1)} %all-gather.4.cloned.1.call-done) | copy-start | bytes 5898244
  92.0 1.3 copy-start.1
  94.8 66.0 %all-gather.8.cloned.1.call-start = ((), (), s32[]{:S(2)}) async-start(), calls=%async_computation.4 | async-start | bytes 1474560 | tf_op jit(solution)/shard_map/all_gather | solution.py:102
  128.8 2.3 copy-start.9
  171.0 212.1 %copy-start.6 = (f32[336]{0:T(512)S(1)}, f32[336]{0:T(512)}, u32[]{:S(2)}) copy-start(f32[336]{0:T(512)} %param.19) | copy-start | bytes 4036
  171.0 212.1 %copy-start.7 = (f32[336]{0:T(512)S(1)}, f32[336]{0:T(512)}, u32[]{:S(2)}) copy-start(f32[336]{0:T(512)} %param.20) | copy-start | bytes 4036
  171.1 212.1 %copy-start.8 = (f32[336]{0:T(512)S(1)}, f32[336]{0:T(512)}, u32[]{:S(2)}) copy-start(f32[336]{0:T(512)} %param.21) | copy-start | bytes 4036
  172.9 211.6 %all-to-all-start.1 = ((bf16[128,2,960]{2,1,0:T(2,128)(2,1)}), bf16[128,2,960]{2,1,0:T(2,128)(2,1)S(1)}, u32[]{:S(2)}, u32[]{:S(2)}) async-start(bf16[128,2,960]{2,1,0:T(2,128)(2,1)} %reshape.50), calls=%async_computation.1 | async-start | bytes 1048576 | tf_op jit(solution)/shard_map/all_to_all | solution.py:141
  189.3 193.8 %all-reduce.3.cloned.1.call-start = ((), (), s32[]{:S(2)}) async-start(), calls=%async_computation.5 | async-start | bytes 344064
  385.3 1.3 copy-start.3
  386.4 1.3 copy-start.4
Sparse Core Ops, SparseCore 0:
  59.1 28.4 all-gather.3
  94.9 27.7 all-gather.5
  130.5 30.3 all-gather.7
Sparse Core Ops, SparseCore 1:
  193.0 190.0 all-reduce.2
where the time goes:
time: 396 us
  waiting for transfers between devices  296 us (75%)
  starting transfers between devices  35.2 us (9%)
  matrix products  20.7 us (5%)
  between operations  17.5 us (4%)
  local copies, waits for them, and re-layouts  14.7 us (4%)
  other arithmetic  12 us (3%)
    unnamed x5, waiting for transfers between devices  192 us
    all_gather x2, waiting for transfers between devices, gather_gram(): return lax.all_gather(gram_part, 'tensor', axis=0, tiled=True)  56.4 us
    all_gather x1, waiting for transfers between devices, gather_columns(): return lax.all_gather(column_part, 'tensor', axis=1, tiled=True)  28.6 us
    all_to_all x1, waiting for transfers between devices, per_device(): lax.all_to_all(route_rows(joint_map, joint_pieces), 'shard', split_axis=0...  18.7 us
    all_to_all x1, starting transfers between devices, per_device(): lax.all_to_all(route_rows(joint_map, joint_pieces), 'shard', split_axis=0...  18.4 us
    dot_general x4, matrix products, newton_step(): lax.dot_general(full_iterate, polynomial, (((1,), (1,)), ((), ())), prefe...  16.4 us
    all_to_all x1, starting transfers between devices, per_device(): lax.all_to_all(own_result.reshape(shards, rows_dev, block_width), 'shard'...  16.4 us
    unnamed x27, local copies, waits for them, and re-layouts  9.48 us
  transfers between devices with their start and end apart: 6, of which 5 were waited for; matrix products, arithmetic and copies ran while one was open for 1% of the time, Pallas kernels for 0%

commit v1 on v0

--- a/solution.py
+++ b/solution.py
@@ -132,11 +132,13 @@
     small_retained, small_blended = advance(arrived, small_moment[0], small_owner)
     small_result = small_newton(small_blended)
     full_iterate = normalized(gather_columns(big_blended))
-    for iteration in range(ITERS):
-        owned_part = lax.dynamic_slice_in_dim(full_iterate, column * block_width, block_width, 1)
-        gram_full = gather_gram(gram_block(owned_part, full_iterate))
+    for iteration in range(ITERS - 1):
+        gram_full = gram_block(full_iterate, full_iterate)
         full_iterate = newton_step(full_iterate, full_iterate, poly_block(gram_full, gram_full))
-    big_result = lax.dynamic_slice_in_dim(full_iterate, column * block_width, block_width, 1)
+    gram_full = gram_block(full_iterate, full_iterate)
+    gram_rows = lax.dynamic_slice_in_dim(gram_full, column * block_width, block_width, 0)
+    owned_part = lax.dynamic_slice_in_dim(full_iterate, column * block_width, block_width, 1)
+    big_result = newton_step(owned_part, full_iterate, poly_block(gram_rows, gram_full))
     own_result = jnp.where(big_owner, big_result, small_result)
     returned = lax.all_to_all(
         own_result.reshape(shards, rows_dev, block_width),
@@ -148,7 +150,10 @@
     picked = collect(joint_map, returned)
     big_weight_new = apply_update(big_weight, picked[:matrices])
     small_weight_new = apply_update(small_weight, picked[matrices:])
-    grad_share = lax.psum_scatter(vec_parts[0], "shard", scatter_dimension=0, tiled=True)
+    vec_pieces = vec_parts[0].reshape(shards, -1)
+    grad_share = jnp.sum(
+        lax.all_to_all(vec_pieces, "shard", split_axis=0, concat_axis=0, tiled=True), axis=0
+    )
     first_new = first_decay * vec_first + (1.0 - first_decay) * grad_share
     second_new = second_decay * vec_second + (1.0 - second_decay) * grad_share * grad_share
     param_new = vec_param - adam_rate * (first_new / first_correct) / (

time: 396 us -> 154 us (0.39)
  waiting for transfers between devices: 296 us -> 53.9 us
  starting transfers between devices: 35.2 us -> 40.2 us
    unnamed x5 -> x1, waiting for transfers between devices: 192 us -> 0.02 us
    all_gather x2 -> x0, waiting for transfers between devices: 56.4 us -> none  [gather_gram(): return lax.all_gather(gram_part, 'tensor', axis=0, tiled=True)]
    all_to_all x1, waiting for transfers between devices: 0.01 us -> 18.6 us  [per_device(): lax.all_to_all(own_result.reshape(shards, rows_dev, block_width), 'shard'...]
    all_gather x1, waiting for transfers between devices: 28.6 us -> 16.5 us  [gather_columns(): return lax.all_gather(column_part, 'tensor', axis=1, tiled=True)]
    all_to_all x0 -> x1, starting transfers between devices: none -> 7.25 us  [per_device(): lax.all_to_all(vec_pieces, 'shard', split_axis=0, concat_axis=0, tiled=True)]
    dot_general x4, matrix products: 16.4 us -> 10.4 us  [newton_step(): lax.dot_general(full_iterate, polynomial, (((1,), (1,)), ((), ())), prefe...]
    unnamed x27 -> x25, local copies, waits for them, and re-layouts: 9.48 us -> 7.42 us
  transfers between devices with their start and end apart: 6 -> 4, of which waited for: 5 -> 3; matrix products, arithmetic and copies ran while one was open for 1% -> 17% of each run, Pallas kernels for 0% -> 0%
where the time goes in v1:
time: 154 us
  waiting for transfers between devices  53.9 us (35%)
  starting transfers between devices  40.2 us (26%)
  matrix products  18.2 us (12%)
  between operations  15.7 us (10%)
  local copies, waits for them, and re-layouts  13.7 us (9%)
  other arithmetic  12.2 us (8%)
    all_to_all x1, waiting for transfers between devices, per_device(): lax.all_to_all(route_rows(joint_map, joint_pieces), 'shard', split_axis=0...  18.7 us
    all_to_all x1, waiting for transfers between devices, per_device(): lax.all_to_all(own_result.reshape(shards, rows_dev, block_width), 'shard'...  18.6 us
    all_to_all x1, starting transfers between devices, per_device(): lax.all_to_all(route_rows(joint_map, joint_pieces), 'shard', split_axis=0...  18.4 us
    all_gather x1, waiting for transfers between devices, gather_columns(): return lax.all_gather(column_part, 'tensor', axis=1, tiled=True)  16.5 us
    all_to_all x1, starting transfers between devices, per_device(): lax.all_to_all(own_result.reshape(shards, rows_dev, block_width), 'shard'...  14.5 us
    dot_general x4, matrix products, newton_step(): lax.dot_general(full_iterate, polynomial, (((1,), (1,)), ((), ())), prefe...  10.4 us
    unnamed x25, local copies, waits for them, and re-layouts  7.42 us
    all_to_all x1, starting transfers between devices, per_device(): lax.all_to_all(vec_pieces, 'shard', split_axis=0, concat_axis=0, tiled=True)  7.25 us
  transfers between devices with their start and end apart: 4, of which 3 were waited for; matrix products, arithmetic and copies ran while one was open for 17% of the time, Pallas kernels for 0%

profile of v1, /device:TPU:1, one launch (start us, length us, event | category | flops | bytes accessed | tf_op | source)
XLA Modules:
  0.0 153.9 jit_solution(12986507688042528019)
XLA Ops:
  7.2 0.8 slice_bitcast_fusion.1
  7.9 1.0 pad_maximum_fusion
  9.2 0.4 reshape.45
  10.2 1.3 copy.34
  11.5 1.6 %reshape.59 = bf16[128,2,960]{2,1,0:T(2,128)(2,1)} reshape(bf16[128,10,192]{2,1,0:T(8,128)(2,1)S(1)} %copy.34) | data formatting | bytes 983040
  13.1 18.4 %all-to-all-start = ((bf16[128,2,960]{2,1,0:T(2,128)(2,1)}), bf16[128,2,960]{2,1,0:T(2,128)(2,1)S(1)}, u32[]{:S(2)}, u32[]{:S(2)}) async-start(bf16[128,2,960]{2,1,0:T(2,128)(2,1)} %reshape.59), calls=%async_computation | async-start | bytes 1048576 | tf_op jit(solution)/shard_map/all_to_all | solution.py:126
  31.6 0.6 compare_reduce_fusion.1
  32.2 18.7 %all-to-all-done = bf16[128,2,960]{2,1,0:T(2,128)(2,1)S(1)} async-done(((bf16[128,2,960]{2,1,0:T(2,128)(2,1)}), bf16[128,2,960]{2,1,0:T(2,128)(2,1)S(1)}, u32[]{:S(2)}, u32[]{:S(2)}) %all-to-all-start) | async-done | bytes 491552 | tf_op jit(solution)/shard_map/all_to_all | solution.py:126
  50.9 0.8 reshape.60
  52.1 0.4 copy.35
  52.5 0.8 copy-done.1
  53.3 4.9 %fusion.17 = (f32[1,192,1280]{2,1,0:T(8,128)}, bf16[1280,192]{0,1:T(8,128)(2,1)}, f32[1,192,1280]{2,1,0:T(8,128)}, f32[]{:T(128)}, bf16[192,1280]{1,0:T(8,128)(2,1)S(1)}) fusion(f32[1,192,1280]{2,1,0:T(8,128)S(1)} %copy-done.1, f32[1280,192]{0,1:T(8,128)S(1)} %copy.35, pred[]{:T(512)} %get-tuple-element.21, f32[1,192,1280]{2,1,0:T(8,128)} %param.16, ...), kind=kLoop, calls=%fused_computation.39 | loop fusion | flops 4177919 | bytes 5898246 | tf_op jit(solution)/shard_map/broadcast_in_dim | solution.py:164
  58.2 0.5 broadcast.71
  58.7 1.0 reduce.5
  59.8 1.0 all_to_all.20
  60.8 7.3 %all-to-all-start.2 = ((f32[128,1,336]{2,1,0:T(1,128)}), f32[128,1,336]{2,1,0:T(1,128)S(1)}, u32[]{:S(2)}, u32[]{:S(2)}) async-start(f32[128,1,336]{2,1,0:T(1,128)} %all_to_all.20), calls=%async_computation.2 | async-start | bytes 393216 | tf_op jit(solution)/shard_map/all_to_all | solution.py:155
  69.1 0.4 fusion.3
  69.8 0.4 fusion.4
  70.3 16.5 %all-gather.2.cloned.1.call-done = bf16[1280,768]{0,1:T(8,128)(2,1)} async-done(((bf16[1280,192]{0,1:T(8,128)(2,1)}), bf16[1280,768]{0,1:T(8,128)(2,1)}) %all-gather.2.cloned.1.call-update) | async-done | bytes 1966096 | tf_op jit(solution)/shard_map/all_gather | solution.py:98
  86.8 3.3 %fusion = f32[]{:T(128)} fusion(bf16[1280,768]{0,1:T(8,128)(2,1)} %all-gather.2.cloned.1.call-done), kind=kLoop, calls=%fused_computation.2 | loop fusion | flops 2949119 | bytes 1966084 | tf_op jit(solution)/shard_map/reduce_sum | solution.py:56
  90.8 2.8 %convolution_convert_fusion.3 = bf16[768,768]{1,0:T(8,128)(2,1)} fusion(bf16[1280,768]{0,1:T(8,128)(2,1)S(1)} %copy-done, f32[]{:T(128)S(6)} %add.66), kind=kOutput, calls=%fused_computation.16 | convolution fusion | flops 1513488384 | bytes 3145732 | tf_op jit(solution)/shard_map/dot_general | solution.py:61
  93.6 6.3 %add_convert_fusion = bf16[1280,768]{0,1:T(8,128)(2,1)} fusion(bf16[768,768]{1,0:T(8,128)(2,1)} %convolution_convert_fusion.3, f32[]{:T(128)S(6)} %add.66, bf16[1280,768]{0,1:T(8,128)(2,1)S(1)} %copy-done), kind=kOutput, calls=%fused_computation.4 | convolution fusion | flops 2428698624 | bytes 5111812 | tf_op jit(solution)/shard_map/dot_general | solution.py:75
  99.9 3.8 %convolution_convert_fusion.2 = bf16[768,768]{1,0:T(8,128)(2,1)S(1)} fusion(bf16[1280,768]{0,1:T(8,128)(2,1)} %add_convert_fusion), kind=kOutput, calls=%fused_computation.15 | convolution fusion | flops 1510539264 | bytes 3145728 | tf_op jit(solution)/shard_map/dot_general | solution.py:61
  103.7 3.2 %fusion.5 = bf16[1280,192]{0,1:T(8,128)(2,1)S(1)} fusion(bf16[1280,192]{0,1:T(8,128)(2,1)S(1)} %fusion.4, bf16[1280,768]{0,1:T(8,128)(2,1)} %add_convert_fusion, bf16[768,768]{1,0:T(8,128)(2,1)S(1)} %convolution_convert_fusion.2, s32[]{:T(128)S(6)} %select_n.39, pred[]{:T(512)} %get-tuple-element.21), kind=kOutput, calls=%fused_computation.11 | convolution fusion | flops 605945856 | bytes 5212160 | tf_op jit(solution)/shard_map/dot_general | solution.py:75
  107.5 1.6 %reshape.61 = bf16[128,2,960]{2,1,0:T(2,128)(2,1)} reshape(bf16[128,10,192]{2,1,0:T(8,128)(2,1)S(1)} %reshape.47) | data formatting | bytes 983040
  109.1 14.5 %all-to-all-start.1 = ((bf16[128,2,960]{2,1,0:T(2,128)(2,1)}), bf16[128,2,960]{2,1,0:T(2,128)(2,1)S(1)}, u32[]{:S(2)}, u32[]{:S(2)}) async-start(bf16[128,2,960]{2,1,0:T(2,128)(2,1)} %reshape.61), calls=%async_computation.1 | async-start | bytes 1048576 | tf_op jit(solution)/shard_map/all_to_all | solution.py:143
  123.7 0.6 divide_subtract_fusion
  124.3 18.6 %all-to-all-done.1 = bf16[128,2,960]{2,1,0:T(2,128)(2,1)S(1)} async-done(((bf16[128,2,960]{2,1,0:T(2,128)(2,1)}), bf16[128,2,960]{2,1,0:T(2,128)(2,1)S(1)}, u32[]{:S(2)}, u32[]{:S(2)}) %all-to-all-start.1) | async-done | bytes 491552 | tf_op jit(solution)/shard_map/all_to_all | solution.py:143
  143.0 0.8 reshape.62
  143.7 0.7 copy.37
  145.2 0.7 copy.40
  146.3 0.7 copy.41
  (36 shorter events, 3.6 us)
Async XLA Ops:
  10.2 21.4 %copy-start.5 = (s32[2,32]{1,0:T(2,128)S(1)}, s32[2,32]{1,0:T(2,128)}, u32[]{:S(2)}) copy-start(s32[2,32]{1,0:T(2,128)} %param.17) | copy-start | bytes 772
  13.1 37.8 %all-to-all-start = ((bf16[128,2,960]{2,1,0:T(2,128)(2,1)}), bf16[128,2,960]{2,1,0:T(2,128)(2,1)S(1)}, u32[]{:S(2)}, u32[]{:S(2)}) async-start(bf16[128,2,960]{2,1,0:T(2,128)(2,1)} %reshape.59), calls=%async_computation | async-start | bytes 1048576 | tf_op jit(solution)/shard_map/all_to_all | solution.py:126
  31.5 55.3 %all-gather.2.cloned.1.call-start = ((), (), s32[]{:S(2)}) async-start(), calls=%async_computation.3 | async-start | bytes 2457600 | tf_op jit(solution)/shard_map/all_gather | solution.py:98
  52.1 1.2 copy-start.1
  53.3 5.4 %copy-start.2 = (f32[1,43008]{1,0:T(1,128)S(1)}, f32[1,43008]{1,0:T(1,128)}, u32[]{:S(2)}) copy-start(f32[1,43008]{1,0:T(1,128)} %param.18) | copy-start | bytes 516100
  60.8 48.3 %all-to-all-start.2 = ((f32[128,1,336]{2,1,0:T(1,128)}), f32[128,1,336]{2,1,0:T(1,128)S(1)}, u32[]{:S(2)}, u32[]{:S(2)}) async-start(f32[128,1,336]{2,1,0:T(1,128)} %all_to_all.20), calls=%async_computation.2 | async-start | bytes 393216 | tf_op jit(solution)/shard_map/all_to_all | solution.py:155
  86.8 4.0 %copy-start = (bf16[1280,768]{0,1:T(8,128)(2,1)S(1)}, bf16[1280,768]{0,1:T(8,128)(2,1)}, u32[]{:S(2)}) copy-start(bf16[1280,768]{0,1:T(8,128)(2,1)} %all-gather.2.cloned.1.call-done) | copy-start | bytes 5898244
  107.2 16.5 %copy-start.6 = (f32[336]{0:T(512)S(1)}, f32[336]{0:T(512)}, u32[]{:S(2)}) copy-start(f32[336]{0:T(512)} %param.19) | copy-start | bytes 4036
  107.2 16.5 %copy-start.7 = (f32[336]{0:T(512)S(1)}, f32[336]{0:T(512)}, u32[]{:S(2)}) copy-start(f32[336]{0:T(512)} %param.20) | copy-start | bytes 4036
  107.2 16.5 %copy-start.8 = (f32[336]{0:T(512)S(1)}, f32[336]{0:T(512)}, u32[]{:S(2)}) copy-start(f32[336]{0:T(512)} %param.21) | copy-start | bytes 4036
  109.1 33.9 %all-to-all-start.1 = ((bf16[128,2,960]{2,1,0:T(2,128)(2,1)}), bf16[128,2,960]{2,1,0:T(2,128)(2,1)S(1)}, u32[]{:S(2)}, u32[]{:S(2)}) async-start(bf16[128,2,960]{2,1,0:T(2,128)(2,1)} %reshape.61), calls=%async_computation.1 | async-start | bytes 1048576 | tf_op jit(solution)/shard_map/all_to_all | solution.py:143
  143.7 1.3 copy-start.3
  144.8 1.3 copy-start.4
Sparse Core Ops, SparseCore 0:
  58.3 28.4 all-gather.1

commit v2 on v1

--- a/solution.py
+++ b/solution.py
@@ -95,7 +95,13 @@
 
 
 def gather_columns(column_part):
-    return lax.all_gather(column_part, "tensor", axis=1, tiled=True)
+    count = lax.axis_size("tensor")
+    blocks = [column_part]
+    for shift in range(1, count):
+        blocks.append(
+            lax.ppermute(column_part, "tensor", [(i, (i + shift) % count) for i in range(count)])
+        )
+    return jnp.concatenate(blocks, axis=1)
 
 
 def gather_gram(gram_part):
@@ -136,8 +142,8 @@
         gram_full = gram_block(full_iterate, full_iterate)
         full_iterate = newton_step(full_iterate, full_iterate, poly_block(gram_full, gram_full))
     gram_full = gram_block(full_iterate, full_iterate)
-    gram_rows = lax.dynamic_slice_in_dim(gram_full, column * block_width, block_width, 0)
-    owned_part = lax.dynamic_slice_in_dim(full_iterate, column * block_width, block_width, 1)
+    gram_rows = gram_full[:block_width]
+    owned_part = full_iterate[:, :block_width]
     big_result = newton_step(owned_part, full_iterate, poly_block(gram_rows, gram_full))
     own_result = jnp.where(big_owner, big_result, small_result)
     returned = lax.all_to_all(

time: 154 us -> 149 us (0.968)
  between operations: 15.7 us -> 2.35 us
  starting transfers between devices: 40.2 us -> 49.1 us
  matrix products: 18.2 us -> 21.5 us
  other arithmetic: 12.2 us -> 10.3 us
  waiting for transfers between devices: 53.9 us -> 52.2 us
    ppermute x0 -> x3, waiting for transfers between devices: none -> 17.4 us  [gather_columns(): lax.ppermute(column_part, 'tensor', [(i, (i + shift) % count) for i in ra...]
    all_gather x1 -> x0, waiting for transfers between devices: 16.5 us -> none  [gather_columns(): return lax.all_gather(column_part, 'tensor', axis=1, tiled=True)]
    ppermute x0 -> x3, starting transfers between devices: none -> 9.5 us  [gather_columns(): lax.ppermute(column_part, 'tensor', [(i, (i + shift) % count) for i in ra...]
    all_to_all x1, waiting for transfers between devices: 18.7 us -> 16.2 us  [per_device(): lax.all_to_all(route_rows(joint_map, joint_pieces), 'shard', split_axis=0...]
    dot_general x4, matrix products: 7.25 us -> 9.61 us  [gram_block(): lax.dot_general(left_part, right_part, (((0,), (0,)), ((), ())), preferre...]
    reduce_sum x1, other arithmetic: 3.3 us -> 1.61 us  [normalized(): squares = jnp.sum(values * values)]
  transfers between devices with their start and end apart: 4 -> 6, of which waited for: 3 -> 5; matrix products, arithmetic and copies ran while one was open for 17% -> 23% of each run, Pallas kernels for 0% -> 0%
where the time goes in v2:
time: 149 us; the launch traced here: 148 us
  waiting for transfers between devices  52.2 us (35%)
  starting transfers between devices  49.1 us (33%)
  matrix products  21.5 us (14%)
  local copies, waits for them, and re-layouts  12.6 us (8%)
  other arithmetic  10.3 us (7%)
  between operations  2.35 us (2%)
    all_to_all x1, waiting for transfers between devices, per_device(): lax.all_to_all(own_result.reshape(shards, rows_dev, block_width), 'shard'...  18.6 us
    all_to_all x1, starting transfers between devices, per_device(): lax.all_to_all(route_rows(joint_map, joint_pieces), 'shard', split_axis=0...  18.4 us
    ppermute x3, waiting for transfers between devices, gather_columns(): lax.ppermute(column_part, 'tensor', [(i, (i + shift) % count) for i in ra...  17.4 us
    all_to_all x1, waiting for transfers between devices, per_device(): lax.all_to_all(route_rows(joint_map, joint_pieces), 'shard', split_axis=0...  16.2 us
    all_to_all x1, starting transfers between devices, per_device(): lax.all_to_all(own_result.reshape(shards, rows_dev, block_width), 'shard'...  14 us
    dot_general x4, matrix products, newton_step(): lax.dot_general(full_iterate, polynomial, (((1,), (1,)), ((), ())), prefe...  11.3 us
    dot_general x4, matrix products, gram_block(): lax.dot_general(left_part, right_part, (((0,), (0,)), ((), ())), preferre...  9.61 us
    ppermute x3, starting transfers between devices, gather_columns(): lax.ppermute(column_part, 'tensor', [(i, (i + shift) % count) for i in ra...  9.5 us
  transfers between devices with their start and end apart: 6, of which 5 were waited for; matrix products, arithmetic and copies ran while one was open for 23% of the time, Pallas kernels for 0%

profile of v2, /device:TPU:1, one launch (start us, length us, event | category | flops | bytes accessed | tf_op | source)
XLA Modules:
  0.0 148.0 jit_solution(15735899365972035281)
XLA Ops:
  0.6 1.0 pad_maximum_fusion.1
  2.9 1.3 copy.34
  4.3 1.6 %reshape.59 = bf16[128,2,960]{2,1,0:T(2,128)(2,1)} reshape(bf16[128,10,192]{2,1,0:T(8,128)(2,1)S(1)} %copy.34) | data formatting | bytes 983040
  5.8 18.4 %all-to-all-start = ((bf16[128,2,960]{2,1,0:T(2,128)(2,1)}), bf16[128,2,960]{2,1,0:T(2,128)(2,1)S(1)}, u32[]{:S(2)}, u32[]{:S(2)}) async-start(bf16[128,2,960]{2,1,0:T(2,128)(2,1)} %reshape.59), calls=%async_computation | async-start | bytes 1048576 | tf_op jit(solution)/shard_map/all_to_all | solution.py:132
  24.8 1.0 reduce.5
  25.8 1.0 all_to_all.20
  26.8 0.6 compare_reduce_fusion.1
  27.5 16.2 %all-to-all-done = bf16[128,2,960]{2,1,0:T(2,128)(2,1)S(1)} async-done(((bf16[128,2,960]{2,1,0:T(2,128)(2,1)}), bf16[128,2,960]{2,1,0:T(2,128)(2,1)S(1)}, u32[]{:S(2)}, u32[]{:S(2)}) %all-to-all-start) | async-done | bytes 491552 | tf_op jit(solution)/shard_map/all_to_all | solution.py:132
  43.7 7.2 %all-to-all-start.2 = ((f32[128,1,336]{2,1,0:T(1,128)}), f32[128,1,336]{2,1,0:T(1,128)S(1)}, u32[]{:S(2)}, u32[]{:S(2)}) async-start(f32[128,1,336]{2,1,0:T(1,128)} %all_to_all.20), calls=%async_computation.2 | async-start | bytes 393216 | tf_op jit(solution)/shard_map/all_to_all | solution.py:161
  50.9 0.8 reshape.60
  52.9 4.7 %fusion.17 = (f32[1,192,1280]{2,1,0:T(8,128)}, bf16[1280,192]{0,1:T(8,128)(2,1)S(1)}, f32[1,192,1280]{2,1,0:T(8,128)}, f32[]{:T(128)}, bf16[192,1280]{1,0:T(8,128)(2,1)}) fusion(f32[1,192,1280]{2,1,0:T(8,128)S(1)} %copy-done, f32[1280,192]{0,1:T(8,128)S(1)} %copy.35, pred[]{:T(512)} %get-tuple-element.21, f32[1,192,1280]{2,1,0:T(8,128)} %param.16, ...), kind=kLoop, calls=%fused_computation.40 | loop fusion | flops 4177919 | bytes 5898246 | tf_op jit(solution)/shard_map/broadcast_in_dim | solution.py:170
  57.6 4.4 %collective-permute-start.2 = (bf16[1280,192]{0,1:T(8,128)(2,1)S(1)}, bf16[1280,192]{0,1:T(8,128)(2,1)S(1)}, u32[]{:S(2)}, u32[]{:S(2)}) collective-permute-start(bf16[1280,192]{0,1:T(8,128)(2,1)S(1)} %get-tuple-element.30), channel_id=1, source_target_pairs={{0,3},{1,0},{2,1},{3,2},{4,7},{5,4},{6,5},{7,6},{8,11},{9,8},{10,9... | collective-permute-start | bytes 1474568 | tf_op jit(solution)/shard_map/ppermute | solution.py:102
  62.0 2.4 %collective-permute-start.1 = (bf16[1280,192]{0,1:T(8,128)(2,1)S(1)}, bf16[1280,192]{0,1:T(8,128)(2,1)S(1)}, u32[]{:S(2)}, u32[]{:S(2)}) collective-permute-start(bf16[1280,192]{0,1:T(8,128)(2,1)S(1)} %get-tuple-element.30), channel_id=1, source_target_pairs={{0,2},{1,3},{2,0},{3,1},{4,6},{5,7},{6,4},{7,5},{8,10},{9,11},{10,... | collective-permute-start | bytes 1474568 | tf_op jit(solution)/shard_map/ppermute | solution.py:102
  64.4 2.7 %collective-permute-start = (bf16[1280,192]{0,1:T(8,128)(2,1)S(1)}, bf16[1280,192]{0,1:T(8,128)(2,1)S(1)}, u32[]{:S(2)}, u32[]{:S(2)}) collective-permute-start(bf16[1280,192]{0,1:T(8,128)(2,1)S(1)} %get-tuple-element.30), channel_id=1, source_target_pairs={{0,1},{1,2},{2,3},{3,0},{4,5},{5,6},{6,7},{7,4},{8,9},{9,10},{10,1... | collective-permute-start | bytes 1474568 | tf_op jit(solution)/shard_map/ppermute | solution.py:102
  67.8 1.5 %convolution_convert_fusion.5 = bf16[192,192]{1,0:T(8,128)(2,1)S(1)} fusion(bf16[192,1280]{1,0:T(8,128)(2,1)} %get-tuple-element.33, f32[]{:T(128)S(6)} %add.69), kind=kOutput, calls=%fused_computation.30 | convolution fusion | flops 95145984 | bytes 565252 | tf_op jit(solution)/shard_map/dot_general | solution.py:61
  69.3 1.6 %fusion.3 = bf16[1280,192]{0,1:T(8,128)(2,1)S(1)} fusion(bf16[192,192]{1,0:T(8,128)(2,1)S(1)} %convolution_convert_fusion.5, f32[]{:T(128)S(6)} %add.69, bf16[192,1280]{1,0:T(8,128)(2,1)} %get-tuple-element.33), kind=kOutput, calls=%fused_computation.9 | convolution fusion | flops 111169536 | bytes 1056772 | tf_op jit(solution)/shard_map/dot_general | solution.py:75
  71.7 0.6 collective-permute-done.2
  72.3 4.6 %collective-permute-done.1 = bf16[1280,192]{0,1:T(8,128)(2,1)S(1)} collective-permute-done((bf16[1280,192]{0,1:T(8,128)(2,1)S(1)}, bf16[1280,192]{0,1:T(8,128)(2,1)S(1)}, u32[]{:S(2)}, u32[]{:S(2)}) %collective-permute-start.1) | collective-permute-done | bytes 491552 | tf_op jit(solution)/shard_map/ppermute | solution.py:102
  76.9 12.1 %collective-permute-done = bf16[1280,192]{0,1:T(8,128)(2,1)S(1)} collective-permute-done((bf16[1280,192]{0,1:T(8,128)(2,1)S(1)}, bf16[1280,192]{0,1:T(8,128)(2,1)S(1)}, u32[]{:S(2)}, u32[]{:S(2)}) %collective-permute-start) | collective-permute-done | bytes 491552 | tf_op jit(solution)/shard_map/ppermute | solution.py:102
  89.1 1.6 %fusion = f32[]{:T(128)} fusion(bf16[1280,192]{0,1:T(8,128)(2,1)S(1)} %collective-permute-done.2, bf16[1280,192]{0,1:T(8,128)(2,1)S(1)} %collective-permute-done.1, bf16[1280,192]{0,1:T(8,128)(2,1)S(1)} %collective-permute-done, bf16[1280,192]{0,1:T(8,128)(2,1)S(1)} %get-tuple-element.30), kind=kLoop, calls=%fused_computation.2 | loop fusion | flops 9830399 | bytes 1966084 | tf_op jit(solution)/shard_map/reduce_sum | solution.py:56
  91.4 2.8 %convolution_convert_fusion.3 = bf16[768,768]{1,0:T(8,128)(2,1)} fusion(f32[]{:T(128)S(6)} %add.62, bf16[1280,192]{0,1:T(8,128)(2,1)S(1)} %collective-permute-done.2, bf16[1280,192]{0,1:T(8,128)(2,1)S(1)} %collective-permute-done.1, bf16[1280,192]{0,1:T(8,128)(2,1)S(1)} %collective-permute-done, bf16[1280,192]{0,1:T(8,128)(2,1)S(1)} %get-tuple-element.30), kind=kOutput, calls=%fused_computation.17 | convolution fusion | flops 1520369664 | bytes 3145732 | tf_op jit(solution)/shard_map/dot_general | solution.py:61
  94.2 6.3 %add_convert_fusion = bf16[1280,768]{0,1:T(8,128)(2,1)} fusion(bf16[768,768]{1,0:T(8,128)(2,1)} %convolution_convert_fusion.3, f32[]{:T(128)S(6)} %add.62, bf16[1280,192]{0,1:T(8,128)(2,1)S(1)} %collective-permute-done.2, bf16[1280,192]{0,1:T(8,128)(2,1)S(1)} %collective-permute-done.1, bf16[1280,192]{0,1:T(8,128)(2,1)S(1)} %collective-permute-done, ...), kind=kOutput, calls=%fused_computation.4 | convolution fusion | flops 2442461184 | bytes 5111812 | tf_op jit(solution)/shard_map/dot_general | solution.py:75
  100.5 5.0 %convolution_convert_fusion.2 = bf16[768,768]{1,0:T(8,128)(2,1)} fusion(bf16[1280,768]{0,1:T(8,128)(2,1)} %add_convert_fusion), kind=kOutput, calls=%fused_computation.16 | convolution fusion | flops 1510539264 | bytes 3145728 | tf_op jit(solution)/shard_map/dot_general | solution.py:61
  105.5 3.0 %fusion.5 = bf16[1280,192]{0,1:T(8,128)(2,1)S(1)} fusion(bf16[1280,192]{0,1:T(8,128)(2,1)S(1)} %fusion.4, bf16[1280,768]{0,1:T(8,128)(2,1)S(1)} %copy-done.8, bf16[768,768]{1,0:T(8,128)(2,1)} %convolution_convert_fusion.2, pred[]{:T(512)} %get-tuple-element.21), kind=kOutput, calls=%fused_computation.11 | convolution fusion | flops 605945856 | bytes 5210624 | tf_op jit(solution)/shard_map/dot_general | solution.py:75
  109.0 1.6 %reshape.61 = bf16[128,2,960]{2,1,0:T(2,128)(2,1)} reshape(bf16[128,10,192]{2,1,0:T(8,128)(2,1)S(1)} %reshape.47) | data formatting | bytes 983040
  110.6 14.0 %all-to-all-start.1 = ((bf16[128,2,960]{2,1,0:T(2,128)(2,1)}), bf16[128,2,960]{2,1,0:T(2,128)(2,1)S(1)}, u32[]{:S(2)}, u32[]{:S(2)}) async-start(bf16[128,2,960]{2,1,0:T(2,128)(2,1)} %reshape.61), calls=%async_computation.1 | async-start | bytes 1048576 | tf_op jit(solution)/shard_map/all_to_all | solution.py:149
  124.7 0.6 divide_subtract_fusion
  125.3 18.6 %all-to-all-done.1 = bf16[128,2,960]{2,1,0:T(2,128)(2,1)S(1)} async-done(((bf16[128,2,960]{2,1,0:T(2,128)(2,1)}), bf16[128,2,960]{2,1,0:T(2,128)(2,1)S(1)}, u32[]{:S(2)}, u32[]{:S(2)}) %all-to-all-start.1) | async-done | bytes 491552 | tf_op jit(solution)/shard_map/all_to_all | solution.py:149
  143.9 0.8 reshape.62
  144.7 0.7 copy.37
  146.2 0.7 copy.40
  147.3 0.7 copy.41
  (39 shorter events, 5.4 us)
Async XLA Ops:
  0.6 1.6 %copy-start.4 = (s32[2,32]{1,0:T(2,128)S(1)}, s32[2,32]{1,0:T(2,128)}, u32[]{:S(2)}) copy-start(s32[2,32]{1,0:T(2,128)} %param.17) | copy-start | bytes 772
  2.9 21.9 %copy-start.1 = (f32[1,43008]{1,0:T(1,128)S(1)}, f32[1,43008]{1,0:T(1,128)}, u32[]{:S(2)}) copy-start(f32[1,43008]{1,0:T(1,128)} %param.18) | copy-start | bytes 516100
  5.8 37.8 %all-to-all-start = ((bf16[128,2,960]{2,1,0:T(2,128)(2,1)}), bf16[128,2,960]{2,1,0:T(2,128)(2,1)S(1)}, u32[]{:S(2)}, u32[]{:S(2)}) async-start(bf16[128,2,960]{2,1,0:T(2,128)(2,1)} %reshape.59), calls=%async_computation | async-start | bytes 1048576 | tf_op jit(solution)/shard_map/all_to_all | solution.py:132
  43.7 66.9 %all-to-all-start.2 = ((f32[128,1,336]{2,1,0:T(1,128)}), f32[128,1,336]{2,1,0:T(1,128)S(1)}, u32[]{:S(2)}, u32[]{:S(2)}) async-start(f32[128,1,336]{2,1,0:T(1,128)} %all_to_all.20), calls=%async_computation.2 | async-start | bytes 393216 | tf_op jit(solution)/shard_map/all_to_all | solution.py:161
  51.7 1.2 copy-start
  57.6 14.7 %collective-permute-start.2 = (bf16[1280,192]{0,1:T(8,128)(2,1)S(1)}, bf16[1280,192]{0,1:T(8,128)(2,1)S(1)}, u32[]{:S(2)}, u32[]{:S(2)}) collective-permute-start(bf16[1280,192]{0,1:T(8,128)(2,1)S(1)} %get-tuple-element.30), channel_id=1, source_target_pairs={{0,3},{1,0},{2,1},{3,2},{4,7},{5,4},{6,5},{7,6},{8,11},{9,8},{10,9... | collective-permute-start | bytes 1474568 | tf_op jit(solution)/shard_map/ppermute | solution.py:102
  62.0 14.9 %collective-permute-start.1 = (bf16[1280,192]{0,1:T(8,128)(2,1)S(1)}, bf16[1280,192]{0,1:T(8,128)(2,1)S(1)}, u32[]{:S(2)}, u32[]{:S(2)}) collective-permute-start(bf16[1280,192]{0,1:T(8,128)(2,1)S(1)} %get-tuple-element.30), channel_id=1, source_target_pairs={{0,2},{1,3},{2,0},{3,1},{4,6},{5,7},{6,4},{7,5},{8,10},{9,11},{10,... | collective-permute-start | bytes 1474568 | tf_op jit(solution)/shard_map/ppermute | solution.py:102
  64.4 24.6 %collective-permute-start = (bf16[1280,192]{0,1:T(8,128)(2,1)S(1)}, bf16[1280,192]{0,1:T(8,128)(2,1)S(1)}, u32[]{:S(2)}, u32[]{:S(2)}) collective-permute-start(bf16[1280,192]{0,1:T(8,128)(2,1)S(1)} %get-tuple-element.30), channel_id=1, source_target_pairs={{0,1},{1,2},{2,3},{3,0},{4,5},{5,6},{6,7},{7,4},{8,9},{9,10},{10,1... | collective-permute-start | bytes 1474568 | tf_op jit(solution)/shard_map/ppermute | solution.py:102
  100.4 5.0 %copy-start.8 = (bf16[1280,768]{0,1:T(8,128)(2,1)S(1)}, bf16[1280,768]{0,1:T(8,128)(2,1)}, u32[]{:S(2)}) copy-start(bf16[1280,768]{0,1:T(8,128)(2,1)} %add_convert_fusion) | copy-start | bytes 5898244
  108.7 16.0 %copy-start.5 = (f32[336]{0:T(512)S(1)}, f32[336]{0:T(512)}, u32[]{:S(2)}) copy-start(f32[336]{0:T(512)} %param.19) | copy-start | bytes 4036
  108.7 16.0 %copy-start.6 = (f32[336]{0:T(512)S(1)}, f32[336]{0:T(512)}, u32[]{:S(2)}) copy-start(f32[336]{0:T(512)} %param.20) | copy-start | bytes 4036
  108.7 16.0 %copy-start.7 = (f32[336]{0:T(512)S(1)}, f32[336]{0:T(512)}, u32[]{:S(2)}) copy-start(f32[336]{0:T(512)} %param.21) | copy-start | bytes 4036
  110.6 33.4 %all-to-all-start.1 = ((bf16[128,2,960]{2,1,0:T(2,128)(2,1)}), bf16[128,2,960]{2,1,0:T(2,128)(2,1)S(1)}, u32[]{:S(2)}, u32[]{:S(2)}) async-start(bf16[128,2,960]{2,1,0:T(2,128)(2,1)} %reshape.61), calls=%async_computation.1 | async-start | bytes 1048576 | tf_op jit(solution)/shard_map/all_to_all | solution.py:149
  144.7 1.3 copy-start.2
  145.8 1.3 copy-start.3

commit v3 on v2

--- a/solution.py
+++ b/solution.py
@@ -96,12 +96,19 @@
 
 def gather_columns(column_part):
     count = lax.axis_size("tensor")
-    blocks = [column_part]
-    for shift in range(1, count):
-        blocks.append(
-            lax.ppermute(column_part, "tensor", [(i, (i + shift) % count) for i in range(count)])
-        )
-    return jnp.concatenate(blocks, axis=1)
+    ahead = [(i, (i + 1) % count) for i in range(count)]
+    behind = [(i, (i - 1) % count) for i in range(count)]
+    from_behind = lax.ppermute(column_part, "tensor", ahead)
+    from_ahead = lax.ppermute(column_part, "tensor", behind)
+    half = column_part.shape[0] // 2
+    far = jnp.concatenate(
+        [
+            lax.ppermute(from_behind[:half], "tensor", ahead),
+            lax.ppermute(from_ahead[half:], "tensor", behind),
+        ],
+        axis=0,
+    )
+    return jnp.concatenate([column_part, from_behind, far, from_ahead], axis=1)
 
 
 def gather_gram(gram_part):
@@ -129,9 +136,24 @@
     matrices = big_grad.shape[0]
     joint_map = owner_table(jnp.concatenate([owners[0], owners[1]]), shards)
     joint_pieces = jnp.concatenate([big_grad, small_grad], axis=0)
-    arrived = lax.all_to_all(
-        route_rows(joint_map, joint_pieces), "shard", split_axis=0, concat_axis=1, tiled=True
-    )[0]
+    routed = route_rows(joint_map, joint_pieces).reshape(shards, -1)
+    vec_values = vec_parts[0]
+    vec_high = lax.reduce_precision(vec_values, exponent_bits=8, mantissa_bits=7)
+    vec_low = vec_values - vec_high
+    outgoing = jnp.concatenate(
+        [
+            routed,
+            vec_high.astype(jnp.bfloat16).reshape(shards, -1),
+            vec_low.astype(jnp.bfloat16).reshape(shards, -1),
+        ],
+        axis=1,
+    )
+    incoming = lax.all_to_all(outgoing, "shard", split_axis=0, concat_axis=0, tiled=True)
+    routed_width = routed.shape[1]
+    vec_width = vec_values.shape[0] // shards
+    arrived = incoming[:, :routed_width].reshape(shards * rows_dev, block_width)
+    vec_in = incoming[:, routed_width:].astype(jnp.float32)
+    grad_share = jnp.sum(vec_in[:, :vec_width] + vec_in[:, vec_width:], axis=0)
     big_owner = jnp.any(owners[0] == shard_place)
     small_owner = jnp.any(owners[1] == shard_place)
     big_retained, big_blended = advance(arrived, big_moment[0], big_owner)
@@ -156,10 +178,6 @@
     picked = collect(joint_map, returned)
     big_weight_new = apply_update(big_weight, picked[:matrices])
     small_weight_new = apply_update(small_weight, picked[matrices:])
-    vec_pieces = vec_parts[0].reshape(shards, -1)
-    grad_share = jnp.sum(
-        lax.all_to_all(vec_pieces, "shard", split_axis=0, concat_axis=0, tiled=True), axis=0
-    )
     first_new = first_decay * vec_first + (1.0 - first_decay) * grad_share
     second_new = second_decay * vec_second + (1.0 - second_decay) * grad_share * grad_share
     param_new = vec_param - adam_rate * (first_new / first_correct) / (

time: 149 us -> 149 us (level)
  other arithmetic: 10.3 us -> 17.3 us
  starting transfers between devices: 49.1 us -> 42.9 us
  matrix products: 21.5 us -> 18 us
  local copies, waits for them, and re-layouts: 12.6 us -> 15.6 us
    ppermute x3 -> x4, waiting for transfers between devices: 17.4 us -> 10.1 us  [the longest x1 5.08 us: gather_columns(): from_ahead = lax.ppermute(column_part, 'tensor', behind)]
    all_to_all x2 -> x1, starting transfers between devices: 25.7 us -> 18.4 us  [per_device(): lax.all_to_all(outgoing, 'shard', split_axis=0, concat_axis=0, tiled=True)]
    all_to_all x2 -> x1, waiting for transfers between devices: 16.2 us -> 23.1 us  [per_device(): lax.all_to_all(outgoing, 'shard', split_axis=0, concat_axis=0, tiled=True)]
    convert_element_type x0 -> x4, other arithmetic: none -> 4.55 us  [the longest x1 4.43 us: normalized(): return (values / (jnp.sqrt(squares) + norm_epsilon)).astype(jnp.bfloat16)]
    ppermute x3 -> x4, starting transfers between devices: 9.5 us -> 13.7 us  [the longest x1 5.32 us: gather_columns(): lax.ppermute(from_ahead[half:], 'tensor', behind)]
    dot_general x4, matrix products: 9.61 us -> 6.27 us  [gram_block(): lax.dot_general(left_part, right_part, (((0,), (0,)), ((), ())), preferre...]
    all_to_all x1, starting transfers between devices: 14 us -> 10.8 us  [per_device(): lax.all_to_all(own_result.reshape(shards, rows_dev, block_width), 'shard'...]
    unnamed x25 -> x23, local copies, waits for them, and re-layouts: 7.06 us -> 8.08 us
  transfers between devices with their start and end apart: 6 -> 6, of which waited for: 5 -> 4; matrix products, arithmetic and copies ran while one was open for 23% -> 3% of each run, Pallas kernels for 0% -> 0%
where the time goes in v3:
time: 149 us; the launch traced here: 148 us
  waiting for transfers between devices  51.9 us (35%)
  starting transfers between devices  42.9 us (29%)
  matrix products  18 us (12%)
  other arithmetic  17.3 us (12%)
  local copies, waits for them, and re-layouts  15.6 us (10%)
  between operations  2.39 us (2%)
    all_to_all x1, waiting for transfers between devices, per_device(): lax.all_to_all(outgoing, 'shard', split_axis=0, concat_axis=0, tiled=True)  23.1 us
    all_to_all x1, waiting for transfers between devices, per_device(): lax.all_to_all(own_result.reshape(shards, rows_dev, block_width), 'shard'...  18.6 us
    all_to_all x1, starting transfers between devices, per_device(): lax.all_to_all(outgoing, 'shard', split_axis=0, concat_axis=0, tiled=True)  18.4 us
    dot_general x4, matrix products, newton_step(): lax.dot_general(full_iterate, polynomial, (((1,), (1,)), ((), ())), prefe...  11.1 us
    all_to_all x1, starting transfers between devices, per_device(): lax.all_to_all(own_result.reshape(shards, rows_dev, block_width), 'shard'...  10.8 us
    unnamed x23, local copies, waits for them, and re-layouts  8.08 us
    dot_general x4, matrix products, gram_block(): lax.dot_general(left_part, right_part, (((0,), (0,)), ((), ())), preferre...  6.27 us
    ppermute x1, starting transfers between devices, gather_columns(): lax.ppermute(from_ahead[half:], 'tensor', behind)  5.32 us
  transfers between devices with their start and end apart: 6, of which 4 were waited for; matrix products, arithmetic and copies ran while one was open for 3% of the time, Pallas kernels for 0%

profile of v3, /device:TPU:1, one launch (start us, length us, event | category | flops | bytes accessed | tf_op | source)
XLA Modules:
  0.0 148.1 jit_solution(5781178549466010299)
XLA Ops:
  0.6 0.8 slice_bitcast_fusion.1
  1.9 2.0 %reduce.4 = f32[43008]{0:T(1024)S(1)} reduce(f32[1,43008]{1,0:T(1,128)} %param.18, f32[]{:T(128)} %broadcast.71), dimensions={0}, to_apply=%param.18.reduce_sub_computation.3 | reduce | bytes 344068 | tf_op args[7]
  4.1 1.0 pad_maximum_fusion.1
  6.9 1.1 reduce.5
  8.0 1.6 %reshape.55 = bf16[128,2,1296]{2,1,0:T(2,128)(2,1)} reshape(bf16[128,2592]{1,0:T(8,128)(2,1)S(1)} %reduce.5) | data formatting | bytes 1327104
  9.6 18.4 %all-to-all-start = ((bf16[128,2,1296]{2,1,0:T(2,128)(2,1)}), bf16[128,2,1296]{2,1,0:T(2,128)(2,1)S(1)}, u32[]{:S(2)}, u32[]{:S(2)}) async-start(bf16[128,2,1296]{2,1,0:T(2,128)(2,1)} %reshape.55), calls=%async_computation | async-start | bytes 1441792 | tf_op jit(solution)/shard_map/all_to_all | solution.py:151
  28.7 23.1 %all-to-all-done = bf16[128,2,1296]{2,1,0:T(2,128)(2,1)S(1)} async-done(((bf16[128,2,1296]{2,1,0:T(2,128)(2,1)}), bf16[128,2,1296]{2,1,0:T(2,128)(2,1)S(1)}, u32[]{:S(2)}, u32[]{:S(2)}) %all-to-all-start) | async-done | bytes 663584 | tf_op jit(solution)/shard_map/all_to_all | solution.py:151
  51.8 0.9 reshape.56
  52.8 1.8 %copy.41 = bf16[128,1,2592]{0,2,1:T(8,128)(2,1)S(1)} copy(bf16[128,1,2592]{2,1,0:T(2,128)(2,1)S(1)} %reshape.56) | data formatting | bytes 1327104 | tf_op jit(solution)/shard_map/all_to_all | solution.py:151
  55.8 5.1 %fusion.17 = (f32[1,192,1280]{2,1,0:T(8,128)}, bf16[1280,192]{0,1:T(8,128)(2,1)S(1)}, f32[1,192,1280]{2,1,0:T(8,128)}, f32[]{:T(128)}, bf16[192,1280]{1,0:T(8,128)(2,1)S(1)}) fusion(f32[1,192,1280]{2,1,0:T(8,128)} %param.13, f32[1280,192]{0,1:T(8,128)S(1)} %copy.43, pred[]{:T(512)} %get-tuple-element.28, f32[1,192,1280]{2,1,0:T(8,128)} %param.16, ...), kind=kLoop, calls=%fused_computation.40 | loop fusion | flops 4177919 | bytes 5898246 | tf_op jit(solution)/shard_map/broadcast_in_dim | solution.py:188
  60.9 4.4 %collective-permute-start.2 = (bf16[1280,192]{0,1:T(8,128)(2,1)S(1)}, bf16[1280,192]{0,1:T(8,128)(2,1)S(1)}, u32[]{:S(2)}, u32[]{:S(2)}) collective-permute-start(bf16[1280,192]{0,1:T(8,128)(2,1)S(1)} %get-tuple-element.37), channel_id=1, source_target_pairs={{0,3},{1,0},{2,1},{3,2},{4,7},{5,4},{6,5},{7,6},{8,11},{9,8},{10,9... | collective-permute-start | bytes 1474568 | tf_op jit(solution)/shard_map/ppermute | solution.py:102
  65.3 1.9 %collective-permute-start = (bf16[1280,192]{0,1:T(8,128)(2,1)S(1)}, bf16[1280,192]{0,1:T(8,128)(2,1)S(1)}, u32[]{:S(2)}, u32[]{:S(2)}) collective-permute-start(bf16[1280,192]{0,1:T(8,128)(2,1)S(1)} %get-tuple-element.37), channel_id=1, source_target_pairs={{0,1},{1,2},{2,3},{3,0},{4,5},{5,6},{6,7},{7,4},{8,9},{9,10},{10,1... | collective-permute-start | bytes 1474568 | tf_op jit(solution)/shard_map/ppermute | solution.py:101
  69.0 5.1 %collective-permute-done.2 = bf16[1280,192]{0,1:T(8,128)(2,1)S(1)} collective-permute-done((bf16[1280,192]{0,1:T(8,128)(2,1)S(1)}, bf16[1280,192]{0,1:T(8,128)(2,1)S(1)}, u32[]{:S(2)}, u32[]{:S(2)}) %collective-permute-start.2) | collective-permute-done | bytes 491552 | tf_op jit(solution)/shard_map/ppermute | solution.py:102
  74.1 5.3 %collective-permute-start.3 = (bf16[640,192]{0,1:T(8,128)(2,1)S(1)}, bf16[640,192]{0,1:T(8,128)(2,1)S(1)}, u32[]{:S(2)}, u32[]{:S(2)}) collective-permute-start(bf16[640,192]{0,1:T(8,128)(2,1)S(1)} %slice.54), channel_id=1, source_target_pairs={{0,3},{1,0},{2,1},{3,2},{4,7},{5,4},{6,5},{7,6},{8,11},{9,8},{10,9... | collective-permute-start | bytes 737288 | tf_op jit(solution)/shard_map/ppermute | solution.py:107
  79.4 0.7 slice.53
  80.2 2.1 %collective-permute-start.1 = (bf16[640,192]{0,1:T(8,128)(2,1)}, bf16[640,192]{0,1:T(8,128)(2,1)S(1)}, u32[]{:S(2)}, u32[]{:S(2)}) collective-permute-start(bf16[640,192]{0,1:T(8,128)(2,1)} %slice.53), channel_id=1, source_target_pairs={{0,1},{1,2},{2,3},{3,0},{4,5},{5,6},{6,7},{7,4},{8,9},{9,10},{10,1... | collective-permute-start | bytes 737288 | tf_op jit(solution)/shard_map/ppermute | solution.py:106
  82.3 1.2 fusion.4
  83.5 5.0 %collective-permute-done.1 = bf16[640,192]{0,1:T(8,128)(2,1)S(1)} collective-permute-done((bf16[640,192]{0,1:T(8,128)(2,1)}, bf16[640,192]{0,1:T(8,128)(2,1)S(1)}, u32[]{:S(2)}, u32[]{:S(2)}) %collective-permute-start.1) | collective-permute-done | bytes 245792 | tf_op jit(solution)/shard_map/ppermute | solution.py:106
  88.5 1.6 %fusion = f32[]{:T(128)} fusion(bf16[1280,192]{0,1:T(8,128)(2,1)S(1)} %collective-permute-done.2, bf16[640,192]{0,1:T(8,128)(2,1)S(1)} %collective-permute-done.3, bf16[640,192]{0,1:T(8,128)(2,1)S(1)} %collective-permute-done.1, bf16[1280,192]{0,1:T(8,128)(2,1)S(1)} %collective-permute-done, bf16[1280,192]{0,1:T(8,128)(2,1)S(1)} %get-tuple-element.37), kind=kLoop, calls=%fused_computation.2 | loop fusion | flops 11796479 | bytes 1966084 | tf_op jit(solution)/shard_map/reduce_sum | solution.py:56
  90.8 4.4 %fusion.1 = bf16[1280,768]{0,1:T(8,128)(2,1)S(1)} fusion(f32[]{:T(128)S(6)} %add.65, bf16[1280,192]{0,1:T(8,128)(2,1)S(1)} %collective-permute-done.2, bf16[640,192]{0,1:T(8,128)(2,1)S(1)} %collective-permute-done.3, bf16[640,192]{0,1:T(8,128)(2,1)S(1)} %collective-permute-done.1, bf16[1280,192]{0,1:T(8,128)(2,1)S(1)} %collective-permute-done, ...), kind=kLoop, calls=%fused_computation.3 | loop fusion | flops 11796480 | bytes 3932164 | tf_op jit(solution)/shard_map/convert_element_type | solution.py:57
  95.3 1.3 copy-done
  96.5 1.7 %convolution_convert_fusion.3 = bf16[768,768]{1,0:T(8,128)(2,1)S(1)} fusion(bf16[1280,768]{0,1:T(8,128)(2,1)S(1)} %fusion.1), kind=kOutput, calls=%fused_computation.17 | convolution fusion | flops 1510539264 | bytes 3145728 | tf_op jit(solution)/shard_map/dot_general | solution.py:61
  98.2 6.3 %add_convert_fusion = bf16[1280,768]{0,1:T(8,128)(2,1)} fusion(bf16[1280,768]{0,1:T(8,128)(2,1)} %copy-done, bf16[768,768]{1,0:T(8,128)(2,1)S(1)} %convolution_convert_fusion.3), kind=kOutput, calls=%fused_computation.4 | convolution fusion | flops 2422800384 | bytes 5111808 | tf_op jit(solution)/shard_map/dot_general | solution.py:75
  104.5 3.9 %convolution_convert_fusion.2 = bf16[768,768]{1,0:T(8,128)(2,1)S(1)} fusion(bf16[1280,768]{0,1:T(8,128)(2,1)} %add_convert_fusion), kind=kOutput, calls=%fused_computation.16 | convolution fusion | flops 1510539264 | bytes 3145728 | tf_op jit(solution)/shard_map/dot_general | solution.py:61
  108.5 3.2 %fusion.5 = bf16[1280,192]{0,1:T(8,128)(2,1)S(1)} fusion(bf16[1280,192]{0,1:T(8,128)(2,1)S(1)} %copy-done.7, bf16[1280,768]{0,1:T(8,128)(2,1)} %add_convert_fusion, bf16[768,768]{1,0:T(8,128)(2,1)S(1)} %convolution_convert_fusion.2, pred[]{:T(512)} %get-tuple-element.28), kind=kOutput, calls=%fused_computation.11 | convolution fusion | flops 605945856 | bytes 5210624 | tf_op jit(solution)/shard_map/dot_general | solution.py:75
  112.2 1.6 %reshape.57 = bf16[128,2,960]{2,1,0:T(2,128)(2,1)} reshape(bf16[128,10,192]{2,1,0:T(8,128)(2,1)S(1)} %reshape.43) | data formatting | bytes 983040
  113.8 10.8 %all-to-all-start.1 = ((bf16[128,2,960]{2,1,0:T(2,128)(2,1)}), bf16[128,2,960]{2,1,0:T(2,128)(2,1)S(1)}, u32[]{:S(2)}, u32[]{:S(2)}) async-start(bf16[128,2,960]{2,1,0:T(2,128)(2,1)} %reshape.57), calls=%async_computation.1 | async-start | bytes 1048576 | tf_op jit(solution)/shard_map/all_to_all | solution.py:171
  125.4 18.6 %all-to-all-done.1 = bf16[128,2,960]{2,1,0:T(2,128)(2,1)S(1)} async-done(((bf16[128,2,960]{2,1,0:T(2,128)(2,1)}), bf16[128,2,960]{2,1,0:T(2,128)(2,1)S(1)}, u32[]{:S(2)}, u32[]{:S(2)}) %all-to-all-start.1) | async-done | bytes 491552 | tf_op jit(solution)/shard_map/all_to_all | solution.py:171
  144.0 0.8 reshape.58
  144.8 0.7 copy.45
  146.3 0.7 copy.48
  147.4 0.7 copy.47
  (46 shorter events, 7.8 us)
Async XLA Ops:
  6.9 21.1 %copy-start.3 = (s32[2,32]{1,0:T(2,128)S(1)}, s32[2,32]{1,0:T(2,128)}, u32[]{:S(2)}) copy-start(s32[2,32]{1,0:T(2,128)} %param.17) | copy-start | bytes 772
  9.6 42.2 %all-to-all-start = ((bf16[128,2,1296]{2,1,0:T(2,128)(2,1)}), bf16[128,2,1296]{2,1,0:T(2,128)(2,1)S(1)}, u32[]{:S(2)}, u32[]{:S(2)}) async-start(bf16[128,2,1296]{2,1,0:T(2,128)(2,1)} %reshape.55), calls=%async_computation | async-start | bytes 1441792 | tf_op jit(solution)/shard_map/all_to_all | solution.py:151
  60.9 13.2 %collective-permute-start.2 = (bf16[1280,192]{0,1:T(8,128)(2,1)S(1)}, bf16[1280,192]{0,1:T(8,128)(2,1)S(1)}, u32[]{:S(2)}, u32[]{:S(2)}) collective-permute-start(bf16[1280,192]{0,1:T(8,128)(2,1)S(1)} %get-tuple-element.37), channel_id=1, source_target_pairs={{0,3},{1,0},{2,1},{3,2},{4,7},{5,4},{6,5},{7,6},{8,11},{9,8},{10,9... | collective-permute-start | bytes 1474568 | tf_op jit(solution)/shard_map/ppermute | solution.py:102
  65.3 14.1 %collective-permute-start = (bf16[1280,192]{0,1:T(8,128)(2,1)S(1)}, bf16[1280,192]{0,1:T(8,128)(2,1)S(1)}, u32[]{:S(2)}, u32[]{:S(2)}) collective-permute-start(bf16[1280,192]{0,1:T(8,128)(2,1)S(1)} %get-tuple-element.37), channel_id=1, source_target_pairs={{0,1},{1,2},{2,3},{3,0},{4,5},{5,6},{6,7},{7,4},{8,9},{9,10},{10,1... | collective-permute-start | bytes 1474568 | tf_op jit(solution)/shard_map/ppermute | solution.py:101
  74.1 9.4 %collective-permute-start.3 = (bf16[640,192]{0,1:T(8,128)(2,1)S(1)}, bf16[640,192]{0,1:T(8,128)(2,1)S(1)}, u32[]{:S(2)}, u32[]{:S(2)}) collective-permute-start(bf16[640,192]{0,1:T(8,128)(2,1)S(1)} %slice.54), channel_id=1, source_target_pairs={{0,3},{1,0},{2,1},{3,2},{4,7},{5,4},{6,5},{7,6},{8,11},{9,8},{10,9... | collective-permute-start | bytes 737288 | tf_op jit(solution)/shard_map/ppermute | solution.py:107
  80.2 8.3 %collective-permute-start.1 = (bf16[640,192]{0,1:T(8,128)(2,1)}, bf16[640,192]{0,1:T(8,128)(2,1)S(1)}, u32[]{:S(2)}, u32[]{:S(2)}) collective-permute-start(bf16[640,192]{0,1:T(8,128)(2,1)} %slice.53), channel_id=1, source_target_pairs={{0,1},{1,2},{2,3},{3,0},{4,5},{5,6},{6,7},{7,4},{8,9},{9,10},{10,1... | collective-permute-start | bytes 737288 | tf_op jit(solution)/shard_map/ppermute | solution.py:106
  95.2 1.3 copy-start
  104.5 3.9 %copy-start.7 = (bf16[1280,192]{0,1:T(8,128)(2,1)S(1)}, bf16[1280,192]{0,1:T(8,128)(2,1)}, u32[]{:S(2)}) copy-start(bf16[1280,192]{0,1:T(8,128)(2,1)} %fusion.4) | copy-start | bytes 1474564
  112.2 12.6 %copy-start.4 = (f32[336]{0:T(512)S(1)}, f32[336]{0:T(512)}, u32[]{:S(2)}) copy-start(f32[336]{0:T(512)} %param.19) | copy-start | bytes 4036
  112.2 12.6 %copy-start.5 = (f32[336]{0:T(512)S(1)}, f32[336]{0:T(512)}, u32[]{:S(2)}) copy-start(f32[336]{0:T(512)} %param.20) | copy-start | bytes 4036
  112.2 12.6 %copy-start.6 = (f32[336]{0:T(512)S(1)}, f32[336]{0:T(512)}, u32[]{:S(2)}) copy-start(f32[336]{0:T(512)} %param.21) | copy-start | bytes 4036
  113.8 30.2 %all-to-all-start.1 = ((bf16[128,2,960]{2,1,0:T(2,128)(2,1)}), bf16[128,2,960]{2,1,0:T(2,128)(2,1)S(1)}, u32[]{:S(2)}, u32[]{:S(2)}) async-start(bf16[128,2,960]{2,1,0:T(2,128)(2,1)} %reshape.57), calls=%async_computation.1 | async-start | bytes 1048576 | tf_op jit(solution)/shard_map/all_to_all | solution.py:171
  144.8 1.3 copy-start.1
  145.9 1.3 copy-start.2

commit v4 on v2

--- a/solution.py
+++ b/solution.py
@@ -94,14 +94,20 @@
     ).astype(jnp.bfloat16)
 
 
-def gather_columns(column_part):
+def gather_columns(column_part, rider):
     count = lax.axis_size("tensor")
-    blocks = [column_part]
-    for shift in range(1, count):
-        blocks.append(
-            lax.ppermute(column_part, "tensor", [(i, (i + shift) % count) for i in range(count)])
-        )
-    return jnp.concatenate(blocks, axis=1)
+    ahead = [(i, (i + 1) % count) for i in range(count)]
+    behind = [(i, (i - 1) % count) for i in range(count)]
+    from_behind = lax.ppermute(column_part, "tensor", ahead)
+    from_ahead = lax.ppermute(column_part, "tensor", behind)
+    from_behind, from_ahead, rider = lax.optimization_barrier((from_behind, from_ahead, rider))
+    half = column_part.shape[1] // 2
+    far_first = lax.ppermute(from_behind[:, :half], "tensor", ahead)
+    far_second = lax.ppermute(from_ahead[:, half:], "tensor", behind)
+    gathered = jnp.concatenate(
+        [column_part, from_behind, far_first, far_second, from_ahead], axis=1
+    )
+    return gathered, rider
 
 
 def gather_gram(gram_part):
@@ -137,7 +143,11 @@
     big_retained, big_blended = advance(arrived, big_moment[0], big_owner)
     small_retained, small_blended = advance(arrived, small_moment[0], small_owner)
     small_result = small_newton(small_blended)
-    full_iterate = normalized(gather_columns(big_blended))
+    gathered, vec_pieces = gather_columns(big_blended, vec_parts[0].reshape(shards, -1))
+    full_iterate = normalized(gathered)
+    grad_share = jnp.sum(
+        lax.all_to_all(vec_pieces, "shard", split_axis=0, concat_axis=0, tiled=True), axis=0
+    )
     for iteration in range(ITERS - 1):
         gram_full = gram_block(full_iterate, full_iterate)
         full_iterate = newton_step(full_iterate, full_iterate, poly_block(gram_full, gram_full))
@@ -156,10 +166,6 @@
     picked = collect(joint_map, returned)
     big_weight_new = apply_update(big_weight, picked[:matrices])
     small_weight_new = apply_update(small_weight, picked[matrices:])
-    vec_pieces = vec_parts[0].reshape(shards, -1)
-    grad_share = jnp.sum(
-        lax.all_to_all(vec_pieces, "shard", split_axis=0, concat_axis=0, tiled=True), axis=0
-    )
     first_new = first_decay * vec_first + (1.0 - first_decay) * grad_share
     second_new = second_decay * vec_second + (1.0 - second_decay) * grad_share * grad_share
     param_new = vec_param - adam_rate * (first_new / first_correct) / (

time: 149 us -> 143 us (0.960)
  waiting for transfers between devices: 52.2 us -> 39.5 us
  starting transfers between devices: 49.1 us -> 54.9 us
  local copies, waits for them, and re-layouts: 12.6 us -> 17.9 us
  matrix products: 21.5 us -> 16.9 us
    ppermute x3 -> x4, waiting for transfers between devices: 17.4 us -> 3.84 us  [the longest x1 2.2 us: gather_columns(): from_behind = lax.ppermute(column_part, 'tensor', ahead)]
    broadcast_in_dim x1 -> x0, other arithmetic: 4.71 us -> none  [per_device(): big_retained[None]]
    reduce_sum x1 -> x2, other arithmetic: 1.61 us -> 5.19 us  [normalized(): squares = jnp.sum(values * values)]
    ppermute x3 -> x4, starting transfers between devices: 9.5 us -> 13 us  [the longest x1 3.39 us: gather_columns(): far_second = lax.ppermute(from_ahead[:, half:], 'tensor', behind)]
    all_to_all x1, starting transfers between devices: 7.25 us -> 9.74 us  [per_device(): lax.all_to_all(vec_pieces, 'shard', split_axis=0, concat_axis=0, tiled=True)]
    dot_general x4, matrix products: 11.3 us -> 8.85 us  [newton_step(): lax.dot_general(full_iterate, polynomial, (((1,), (1,)), ((), ())), prefe...]
    dot_general x4, matrix products: 9.61 us -> 7.44 us  [gram_block(): lax.dot_general(left_part, right_part, (((0,), (0,)), ((), ())), preferre...]
    slice x0 -> x2, local copies, waits for them, and re-layouts: none -> 1.92 us  [the longest x1 0.96 us: gather_columns(): far_first = lax.ppermute(from_behind[:, :half], 'tensor', ahead)]
  transfers between devices with their start and end apart: 6 -> 7, of which waited for: 5 -> 4; matrix products, arithmetic and copies ran while one was open for 23% -> 22% of each run, Pallas kernels for 0% -> 0%
where the time goes in v4:
time: 143 us
  starting transfers between devices  54.9 us (38%)
  waiting for transfers between devices  39.5 us (28%)
  local copies, waits for them, and re-layouts  17.9 us (13%)
  matrix products  16.9 us (12%)
  other arithmetic  10.9 us (8%)
  between operations  2.43 us (2%)
    all_to_all x1, waiting for transfers between devices, per_device(): lax.all_to_all(own_result.reshape(shards, rows_dev, block_width), 'shard'...  18.6 us
    all_to_all x1, starting transfers between devices, per_device(): lax.all_to_all(route_rows(joint_map, joint_pieces), 'shard', split_axis=0...  18.4 us
    all_to_all x1, waiting for transfers between devices, per_device(): lax.all_to_all(route_rows(joint_map, joint_pieces), 'shard', split_axis=0...  17 us
    all_to_all x1, starting transfers between devices, per_device(): lax.all_to_all(own_result.reshape(shards, rows_dev, block_width), 'shard'...  13.7 us
    all_to_all x1, starting transfers between devices, per_device(): lax.all_to_all(vec_pieces, 'shard', split_axis=0, concat_axis=0, tiled=True)  9.74 us
    dot_general x4, matrix products, newton_step(): lax.dot_general(full_iterate, polynomial, (((1,), (1,)), ((), ())), prefe...  8.85 us
    unnamed x34, local copies, waits for them, and re-layouts  8.6 us
    dot_general x4, matrix products, gram_block(): lax.dot_general(left_part, right_part, (((0,), (0,)), ((), ())), preferre...  7.44 us
  transfers between devices with their start and end apart: 7, of which 4 were waited for; matrix products, arithmetic and copies ran while one was open for 22% of the time, Pallas kernels for 0%

profile of v4, /device:TPU:1, one launch (start us, length us, event | category | flops | bytes accessed | tf_op | source)
XLA Modules:
  0.0 142.5 jit_solution(16339350063394648367)
XLA Ops:
  0.6 0.8 slice_bitcast_fusion.1
  1.4 1.0 pad_maximum_fusion
  3.7 1.3 copy.34
  5.1 1.6 %reshape.58 = bf16[128,2,960]{2,1,0:T(2,128)(2,1)} reshape(bf16[128,10,192]{2,1,0:T(8,128)(2,1)S(1)} %copy.34) | data formatting | bytes 983040
  6.7 18.4 %all-to-all-start = ((bf16[128,2,960]{2,1,0:T(2,128)(2,1)}), bf16[128,2,960]{2,1,0:T(2,128)(2,1)S(1)}, u32[]{:S(2)}, u32[]{:S(2)}) async-start(bf16[128,2,960]{2,1,0:T(2,128)(2,1)} %reshape.58), calls=%async_computation | async-start | bytes 1048576 | tf_op jit(solution)/shard_map/all_to_all | solution.py:138
  25.6 1.0 reduce.5
  27.5 17.0 %all-to-all-done = bf16[128,2,960]{2,1,0:T(2,128)(2,1)S(1)} async-done(((bf16[128,2,960]{2,1,0:T(2,128)(2,1)}), bf16[128,2,960]{2,1,0:T(2,128)(2,1)S(1)}, u32[]{:S(2)}, u32[]{:S(2)}) %all-to-all-start) | async-done | bytes 491552 | tf_op jit(solution)/shard_map/all_to_all | solution.py:138
  44.5 0.8 reshape.59
  46.0 0.8 copy-done
  46.8 1.8 %constant_dynamic-update-slice_fusion.4 = (bf16[1280,768]{0,1:T(8,128)(2,1)}, bf16[1280,192]{0,1:T(8,128)(2,1)}) fusion(f32[1,192,1280]{2,1,0:T(8,128)S(1)} %copy-done, f32[1280,192]{0,1:T(8,128)S(1)} %copy.35, pred[]{:T(512)} %get-tuple-element.27), kind=kLoop, calls=%fused_computation.81 | loop fusion | flops 1474559 | bytes 2949121
  48.6 3.1 %collective-permute-start = (bf16[1280,192]{0,1:T(8,128)(2,1)}, bf16[1280,192]{0,1:T(8,128)(2,1)}, u32[]{:S(2)}, u32[]{:S(2)}) collective-permute-start(bf16[1280,192]{0,1:T(8,128)(2,1)} %get-tuple-element.33), channel_id=1, source_target_pairs={{0,1},{1,2},{2,3},{3,0},{4,5},{5,6},{6,7},{7,4},{8,9},{9,10},{10,1... | collective-permute-start | bytes 1474568 | tf_op jit(solution)/shard_map/ppermute | solution.py:101
  51.7 3.4 %collective-permute-start.1 = (bf16[1280,192]{0,1:T(8,128)(2,1)}, bf16[1280,192]{0,1:T(8,128)(2,1)}, u32[]{:S(2)}, u32[]{:S(2)}) collective-permute-start(bf16[1280,192]{0,1:T(8,128)(2,1)} %get-tuple-element.33), channel_id=1, source_target_pairs={{0,3},{1,0},{2,1},{3,2},{4,7},{5,4},{6,5},{7,6},{8,11},{9,8},{10,9... | collective-permute-start | bytes 1474568 | tf_op jit(solution)/shard_map/ppermute | solution.py:102
  55.1 3.6 %fusion.12 = (f32[]{:T(128)}, bf16[192,1280]{1,0:T(8,128)(2,1)S(1)}, f32[1,192,1280]{2,1,0:T(8,128)}, f32[1,192,1280]{2,1,0:T(8,128)}) fusion(f32[1,192,1280]{2,1,0:T(8,128)S(1)} %copy-done.2, f32[1280,192]{0,1:T(8,128)S(1)} %copy.35, pred[]{:T(512)} %get-tuple-element.28, f32[1,192,1280]{2,1,0:T(8,128)S(1)} %copy-done, pred[]{:T(512)} %get-tuple-element.27), kind=kLoop, calls=%fused_computation.30 | loop fusion | flops 3194879 | bytes 5406726 | tf_op jit(solution)/shard_map/reduce_sum | solution.py:56
  60.5 2.2 %collective-permute-done = bf16[1280,192]{0,1:T(8,128)(2,1)} collective-permute-done((bf16[1280,192]{0,1:T(8,128)(2,1)}, bf16[1280,192]{0,1:T(8,128)(2,1)}, u32[]{:S(2)}, u32[]{:S(2)}) %collective-permute-start) | collective-permute-done | bytes 491552 | tf_op jit(solution)/shard_map/ppermute | solution.py:101
  62.7 1.6 %collective-permute-done.1 = bf16[1280,192]{0,1:T(8,128)(2,1)} collective-permute-done((bf16[1280,192]{0,1:T(8,128)(2,1)}, bf16[1280,192]{0,1:T(8,128)(2,1)}, u32[]{:S(2)}, u32[]{:S(2)}) %collective-permute-start.1) | collective-permute-done | bytes 491552 | tf_op jit(solution)/shard_map/ppermute | solution.py:102
  64.4 1.0 slice.30
  65.3 3.1 %collective-permute-start.2 = (bf16[1280,96]{0,1:T(8,128)(2,1)S(1)}, bf16[1280,96]{0,1:T(8,128)(2,1)S(1)}, u32[]{:S(2)}, u32[]{:S(2)}) collective-permute-start(bf16[1280,96]{0,1:T(8,128)(2,1)S(1)} %slice.30), channel_id=1, source_target_pairs={{0,1},{1,2},{2,3},{3,0},{4,5},{5,6},{6,7},{7,4},{8,9},{9,10},{10,1... | collective-permute-start | bytes 737288 | tf_op jit(solution)/shard_map/ppermute | solution.py:105
  68.5 1.2 fusion.4
  69.7 1.0 slice.31
  70.6 3.4 %collective-permute-start.3 = (bf16[1280,96]{0,1:T(8,128)(2,1)S(1)}, bf16[1280,96]{0,1:T(8,128)(2,1)S(1)}, u32[]{:S(2)}, u32[]{:S(2)}) collective-permute-start(bf16[1280,96]{0,1:T(8,128)(2,1)S(1)} %slice.31), channel_id=1, source_target_pairs={{0,3},{1,0},{2,1},{3,2},{4,7},{5,4},{6,5},{7,6},{8,11},{9,8},{10,9... | collective-permute-start | bytes 737288 | tf_op jit(solution)/shard_map/ppermute | solution.py:106
  74.1 1.1 constant_dynamic-update-slice_fusion.3
  75.1 0.9 copy.39
  76.0 9.7 %all-to-all-start.2 = ((f32[128,1,336]{2,1,0:T(1,128)}), f32[128,1,336]{2,1,0:T(1,128)S(1)}, u32[]{:S(2)}, u32[]{:S(2)}) async-start(f32[128,1,336]{2,1,0:T(1,128)} %copy.39), calls=%async_computation.2 | async-start | bytes 393216 | tf_op jit(solution)/shard_map/all_to_all | solution.py:149
  85.8 1.1 constant_dynamic-update-slice_fusion
  86.9 1.6 %fusion = f32[]{:T(128)} fusion(bf16[1280,768]{0,1:T(8,128)(2,1)S(1)} %constant_dynamic-update-slice_fusion), kind=kLoop, calls=%fused_computation.2 | loop fusion | flops 2949119 | bytes 1966084 | tf_op jit(solution)/shard_map/reduce_sum | solution.py:56
  89.2 1.8 %convolution_convert_fusion.3 = bf16[768,768]{1,0:T(8,128)(2,1)S(1)} fusion(bf16[1280,768]{0,1:T(8,128)(2,1)S(1)} %constant_dynamic-update-slice_fusion, f32[]{:T(128)S(6)} %add.62), kind=kOutput, calls=%fused_computation.16 | convolution fusion | flops 1513488384 | bytes 3145732 | tf_op jit(solution)/shard_map/dot_general | solution.py:61
  90.9 4.2 %add_convert_fusion = bf16[1280,768]{0,1:T(8,128)(2,1)} fusion(bf16[768,768]{1,0:T(8,128)(2,1)S(1)} %convolution_convert_fusion.3, f32[]{:T(128)S(6)} %add.62, bf16[1280,768]{0,1:T(8,128)(2,1)S(1)} %constant_dynamic-update-slice_fusion), kind=kOutput, calls=%fused_computation.4 | convolution fusion | flops 2428698624 | bytes 5111812 | tf_op jit(solution)/shard_map/dot_general | solution.py:75
  95.1 5.0 %convolution_convert_fusion.2 = bf16[768,768]{1,0:T(8,128)(2,1)} fusion(bf16[1280,768]{0,1:T(8,128)(2,1)} %add_convert_fusion), kind=kOutput, calls=%fused_computation.15 | convolution fusion | flops 1510539264 | bytes 3145728 | tf_op jit(solution)/shard_map/dot_general | solution.py:61
  100.2 3.0 %fusion.5 = bf16[1280,192]{0,1:T(8,128)(2,1)S(1)} fusion(bf16[1280,192]{0,1:T(8,128)(2,1)S(1)} %copy-done.10, bf16[1280,768]{0,1:T(8,128)(2,1)S(1)} %copy-done.11, bf16[768,768]{1,0:T(8,128)(2,1)} %convolution_convert_fusion.2, pred[]{:T(512)} %get-tuple-element.27), kind=kOutput, calls=%fused_computation.11 | convolution fusion | flops 605945856 | bytes 5210624 | tf_op jit(solution)/shard_map/dot_general | solution.py:75
  103.7 1.6 %reshape.60 = bf16[128,2,960]{2,1,0:T(2,128)(2,1)} reshape(bf16[128,10,192]{2,1,0:T(8,128)(2,1)S(1)} %reshape.46) | data formatting | bytes 983040
  105.3 13.7 %all-to-all-start.1 = ((bf16[128,2,960]{2,1,0:T(2,128)(2,1)}), bf16[128,2,960]{2,1,0:T(2,128)(2,1)S(1)}, u32[]{:S(2)}, u32[]{:S(2)}) async-start(bf16[128,2,960]{2,1,0:T(2,128)(2,1)} %reshape.60), calls=%async_computation.1 | async-start | bytes 1048576 | tf_op jit(solution)/shard_map/all_to_all | solution.py:159
  119.8 18.6 %all-to-all-done.1 = bf16[128,2,960]{2,1,0:T(2,128)(2,1)S(1)} async-done(((bf16[128,2,960]{2,1,0:T(2,128)(2,1)}), bf16[128,2,960]{2,1,0:T(2,128)(2,1)S(1)}, u32[]{:S(2)}, u32[]{:S(2)}) %all-to-all-start.1) | async-done | bytes 491552 | tf_op jit(solution)/shard_map/all_to_all | solution.py:159
  (55 shorter events, 9.7 us)
Async XLA Ops:
  3.7 21.9 %copy-start.3 = (f32[1,43008]{1,0:T(1,128)S(1)}, f32[1,43008]{1,0:T(1,128)}, u32[]{:S(2)}) copy-start(f32[1,43008]{1,0:T(1,128)} %param.18) | copy-start | bytes 516100
  5.0 21.8 %copy-start.6 = (s32[2,32]{1,0:T(2,128)S(1)}, s32[2,32]{1,0:T(2,128)}, u32[]{:S(2)}) copy-start(s32[2,32]{1,0:T(2,128)} %param.17) | copy-start | bytes 772
  6.7 37.8 %all-to-all-start = ((bf16[128,2,960]{2,1,0:T(2,128)(2,1)}), bf16[128,2,960]{2,1,0:T(2,128)(2,1)S(1)}, u32[]{:S(2)}, u32[]{:S(2)}) async-start(bf16[128,2,960]{2,1,0:T(2,128)(2,1)} %reshape.58), calls=%async_computation | async-start | bytes 1048576 | tf_op jit(solution)/shard_map/all_to_all | solution.py:138
  45.6 1.2 copy-start
  46.0 9.1 %copy-start.2 = (f32[1,192,1280]{2,1,0:T(8,128)S(1)}, f32[1,192,1280]{2,1,0:T(8,128)}, u32[]{:S(2)}) copy-start(f32[1,192,1280]{2,1,0:T(8,128)} %param.16) | copy-start | bytes 2949124
  48.6 14.1 %collective-permute-start = (bf16[1280,192]{0,1:T(8,128)(2,1)}, bf16[1280,192]{0,1:T(8,128)(2,1)}, u32[]{:S(2)}, u32[]{:S(2)}) collective-permute-start(bf16[1280,192]{0,1:T(8,128)(2,1)} %get-tuple-element.33), channel_id=1, source_target_pairs={{0,1},{1,2},{2,3},{3,0},{4,5},{5,6},{6,7},{7,4},{8,9},{9,10},{10,1... | collective-permute-start | bytes 1474568 | tf_op jit(solution)/shard_map/ppermute | solution.py:101
  51.7 12.6 %collective-permute-start.1 = (bf16[1280,192]{0,1:T(8,128)(2,1)}, bf16[1280,192]{0,1:T(8,128)(2,1)}, u32[]{:S(2)}, u32[]{:S(2)}) collective-permute-start(bf16[1280,192]{0,1:T(8,128)(2,1)} %get-tuple-element.33), channel_id=1, source_target_pairs={{0,3},{1,0},{2,1},{3,2},{4,7},{5,4},{6,5},{7,6},{8,11},{9,8},{10,9... | collective-permute-start | bytes 1474568 | tf_op jit(solution)/shard_map/ppermute | solution.py:102
  60.2 13.8 %copy-start.1 = (bf16[1280,768]{0,1:T(8,128)(2,1)S(1)}, bf16[1280,768]{0,1:T(8,128)(2,1)}, u32[]{:S(2)}) copy-start(bf16[1280,768]{0,1:T(8,128)(2,1)} %get-tuple-element.32) | copy-start | bytes 5898244
  65.3 20.4 %collective-permute-start.2 = (bf16[1280,96]{0,1:T(8,128)(2,1)S(1)}, bf16[1280,96]{0,1:T(8,128)(2,1)S(1)}, u32[]{:S(2)}, u32[]{:S(2)}) collective-permute-start(bf16[1280,96]{0,1:T(8,128)(2,1)S(1)} %slice.30), channel_id=1, source_target_pairs={{0,1},{1,2},{2,3},{3,0},{4,5},{5,6},{6,7},{7,4},{8,9},{9,10},{10,1... | collective-permute-start | bytes 737288 | tf_op jit(solution)/shard_map/ppermute | solution.py:105
  70.6 15.1 %collective-permute-start.3 = (bf16[1280,96]{0,1:T(8,128)(2,1)S(1)}, bf16[1280,96]{0,1:T(8,128)(2,1)S(1)}, u32[]{:S(2)}, u32[]{:S(2)}) collective-permute-start(bf16[1280,96]{0,1:T(8,128)(2,1)S(1)} %slice.31), channel_id=1, source_target_pairs={{0,3},{1,0},{2,1},{3,2},{4,7},{5,4},{6,5},{7,6},{8,11},{9,8},{10,9... | collective-permute-start | bytes 737288 | tf_op jit(solution)/shard_map/ppermute | solution.py:106
  76.0 29.3 %all-to-all-start.2 = ((f32[128,1,336]{2,1,0:T(1,128)}), f32[128,1,336]{2,1,0:T(1,128)S(1)}, u32[]{:S(2)}, u32[]{:S(2)}) async-start(f32[128,1,336]{2,1,0:T(1,128)} %copy.39), calls=%async_computation.2 | async-start | bytes 393216 | tf_op jit(solution)/shard_map/all_to_all | solution.py:149
  95.1 5.1 %copy-start.10 = (bf16[1280,192]{0,1:T(8,128)(2,1)S(1)}, bf16[1280,192]{0,1:T(8,128)(2,1)}, u32[]{:S(2)}) copy-start(bf16[1280,192]{0,1:T(8,128)(2,1)} %fusion.4) | copy-start | bytes 1474564
  95.1 5.1 %copy-start.11 = (bf16[1280,768]{0,1:T(8,128)(2,1)S(1)}, bf16[1280,768]{0,1:T(8,128)(2,1)}, u32[]{:S(2)}) copy-start(bf16[1280,768]{0,1:T(8,128)(2,1)} %add_convert_fusion) | copy-start | bytes 5898244
  103.4 15.8 %copy-start.7 = (f32[336]{0:T(512)S(1)}, f32[336]{0:T(512)}, u32[]{:S(2)}) copy-start(f32[336]{0:T(512)} %param.19) | copy-start | bytes 4036
  103.4 15.8 %copy-start.8 = (f32[336]{0:T(512)S(1)}, f32[336]{0:T(512)}, u32[]{:S(2)}) copy-start(f32[336]{0:T(512)} %param.20) | copy-start | bytes 4036
  103.4 15.8 %copy-start.9 = (f32[336]{0:T(512)S(1)}, f32[336]{0:T(512)}, u32[]{:S(2)}) copy-start(f32[336]{0:T(512)} %param.21) | copy-start | bytes 4036
  105.3 33.2 %all-to-all-start.1 = ((bf16[128,2,960]{2,1,0:T(2,128)(2,1)}), bf16[128,2,960]{2,1,0:T(2,128)(2,1)S(1)}, u32[]{:S(2)}, u32[]{:S(2)}) async-start(bf16[128,2,960]{2,1,0:T(2,128)(2,1)} %reshape.60), calls=%async_computation.1 | async-start | bytes 1048576 | tf_op jit(solution)/shard_map/all_to_all | solution.py:159
  139.2 1.3 copy-start.4
  140.3 1.3 copy-start.5

commit v5 on v4

--- a/solution.py
+++ b/solution.py
@@ -46,9 +46,14 @@
 def advance(arrived, moment, is_owner):
     gradient = arrived.T.astype(jnp.float32)
     renewed = momentum_rate * moment + gradient
-    retained = jnp.where(is_owner, renewed, moment)
     blended = jnp.where(is_owner, gradient + momentum_rate * renewed, 0.0).astype(jnp.bfloat16).T
-    return (retained, blended)
+    return blended
+
+
+def retain(arrived, moment, is_owner):
+    arrived, moment = lax.optimization_barrier((arrived, moment))
+    renewed = momentum_rate * moment + arrived.T.astype(jnp.float32)
+    return jnp.where(is_owner, renewed, moment)
 
 
 def normalized(field):
@@ -140,8 +145,10 @@
     )[0]
     big_owner = jnp.any(owners[0] == shard_place)
     small_owner = jnp.any(owners[1] == shard_place)
-    big_retained, big_blended = advance(arrived, big_moment[0], big_owner)
-    small_retained, small_blended = advance(arrived, small_moment[0], small_owner)
+    big_blended = advance(arrived, big_moment[0], big_owner)
+    small_blended = advance(arrived, small_moment[0], small_owner)
+    big_retained = retain(arrived, big_moment[0], big_owner)
+    small_retained = retain(arrived, small_moment[0], small_owner)
     small_result = small_newton(small_blended)
     gathered, vec_pieces = gather_columns(big_blended, vec_parts[0].reshape(shards, -1))
     full_iterate = normalized(gathered)

time: 143 us -> 150 us (1.049)
  waiting for transfers between devices: 39.5 us -> 32.3 us
  matrix products: 16.9 us -> 24 us
  other arithmetic: 10.9 us -> 16.5 us
    all_to_all x1, waiting for transfers between devices: 18.6 us -> 12.5 us  [per_device(): lax.all_to_all(own_result.reshape(shards, rows_dev, block_width), 'shard'...]
    broadcast_in_dim x0 -> x1, other arithmetic: none -> 4.03 us  [per_device(): small_retained[None]]
    dot_general x4, matrix products: 8.85 us -> 12.8 us  [newton_step(): lax.dot_general(full_iterate, polynomial, (((1,), (1,)), ((), ())), prefe...]
    dot_general x4, matrix products: 7.44 us -> 10.6 us  [gram_block(): lax.dot_general(left_part, right_part, (((0,), (0,)), ((), ())), preferre...]
    optimization_barrier x0 -> x2, local copies, waits for them, and re-layouts: none -> 2.02 us  [retain(): arrived, moment = lax.optimization_barrier((arrived, moment))]
    unnamed x34 -> x30, local copies, waits for them, and re-layouts: 8.6 us -> 9.83 us
  transfers between devices with their start and end apart: 7 -> 7, of which waited for: 4 -> 4; matrix products, arithmetic and copies ran while one was open for 22% -> 30% of each run, Pallas kernels for 0% -> 0%
where the time goes in v5:
time: 150 us; the launch traced here: 149 us
  starting transfers between devices  55 us (37%)
  waiting for transfers between devices  32.3 us (22%)
  matrix products  24 us (16%)
  local copies, waits for them, and re-layouts  18.8 us (13%)
  other arithmetic  16.5 us (11%)
  between operations  2.37 us (2%)
    all_to_all x1, starting transfers between devices, per_device(): lax.all_to_all(route_rows(joint_map, joint_pieces), 'shard', split_axis=0...  18.4 us
    all_to_all x1, waiting for transfers between devices, per_device(): lax.all_to_all(route_rows(joint_map, joint_pieces), 'shard', split_axis=0...  17 us
    all_to_all x1, starting transfers between devices, per_device(): lax.all_to_all(own_result.reshape(shards, rows_dev, block_width), 'shard'...  13.9 us
    dot_general x4, matrix products, newton_step(): lax.dot_general(full_iterate, polynomial, (((1,), (1,)), ((), ())), prefe...  12.8 us
    all_to_all x1, waiting for transfers between devices, per_device(): lax.all_to_all(own_result.reshape(shards, rows_dev, block_width), 'shard'...  12.5 us
    dot_general x4, matrix products, gram_block(): lax.dot_general(left_part, right_part, (((0,), (0,)), ((), ())), preferre...  10.6 us
    unnamed x30, local copies, waits for them, and re-layouts  9.83 us
    all_to_all x1, starting transfers between devices, per_device(): lax.all_to_all(vec_pieces, 'shard', split_axis=0, concat_axis=0, tiled=True)  9.74 us
  transfers between devices with their start and end apart: 7, of which 4 were waited for; matrix products, arithmetic and copies ran while one was open for 30% of the time, Pallas kernels for 0%

profile of v5, /device:TPU:1, one launch (start us, length us, event | category | flops | bytes accessed | tf_op | source)
XLA Modules:
  0.0 149.0 jit_solution(1167730670504329555)
XLA Ops:
  0.6 1.0 pad_maximum_fusion
  2.9 1.3 copy.36
  4.3 1.6 %reshape.55 = bf16[128,2,960]{2,1,0:T(2,128)(2,1)} reshape(bf16[128,10,192]{2,1,0:T(8,128)(2,1)S(1)} %copy.36) | data formatting | bytes 983040
  5.8 18.4 %all-to-all-start = ((bf16[128,2,960]{2,1,0:T(2,128)(2,1)}), bf16[128,2,960]{2,1,0:T(2,128)(2,1)S(1)}, u32[]{:S(2)}, u32[]{:S(2)}) async-start(bf16[128,2,960]{2,1,0:T(2,128)(2,1)} %reshape.55), calls=%async_computation | async-start | bytes 1048576 | tf_op jit(solution)/shard_map/all_to_all | solution.py:143
  24.8 1.0 reduce.5
  26.6 17.0 %all-to-all-done = bf16[128,2,960]{2,1,0:T(2,128)(2,1)S(1)} async-done(((bf16[128,2,960]{2,1,0:T(2,128)(2,1)}), bf16[128,2,960]{2,1,0:T(2,128)(2,1)S(1)}, u32[]{:S(2)}, u32[]{:S(2)}) %all-to-all-start) | async-done | bytes 491552 | tf_op jit(solution)/shard_map/all_to_all | solution.py:143
  45.1 3.1 %constant_dynamic-update-slice_fusion.4 = (bf16[1280,768]{0,1:T(8,128)(2,1)}, bf16[1280,192]{0,1:T(8,128)(2,1)}) fusion(f32[1,192,1280]{2,1,0:T(8,128)} %param.13, bf16[1280,192]{0,1:T(8,128)(2,1)S(1)} %copy.37, pred[]{:T(512)} %get-tuple-element.35), kind=kLoop, calls=%fused_computation.83 | loop fusion | flops 1720319 | bytes 2457601
  48.2 3.1 %collective-permute-start = (bf16[1280,192]{0,1:T(8,128)(2,1)}, bf16[1280,192]{0,1:T(8,128)(2,1)S(1)}, u32[]{:S(2)}, u32[]{:S(2)}) collective-permute-start(bf16[1280,192]{0,1:T(8,128)(2,1)} %get-tuple-element.41), channel_id=1, source_target_pairs={{0,1},{1,2},{2,3},{3,0},{4,5},{5,6},{6,7},{7,4},{8,9},{9,10},{10,1... | collective-permute-start | bytes 1474568 | tf_op jit(solution)/shard_map/ppermute | solution.py:106
  51.3 3.4 %collective-permute-start.1 = (bf16[1280,192]{0,1:T(8,128)(2,1)}, bf16[1280,192]{0,1:T(8,128)(2,1)S(1)}, u32[]{:S(2)}, u32[]{:S(2)}) collective-permute-start(bf16[1280,192]{0,1:T(8,128)(2,1)} %get-tuple-element.41), channel_id=1, source_target_pairs={{0,3},{1,0},{2,1},{3,2},{4,7},{5,4},{6,5},{7,6},{8,11},{9,8},{10,9... | collective-permute-start | bytes 1474568 | tf_op jit(solution)/shard_map/ppermute | solution.py:107
  54.7 2.3 %fusion.12 = (f32[]{:T(128)}, bf16[192,1280]{1,0:T(8,128)(2,1)}) fusion(f32[1,192,1280]{2,1,0:T(8,128)S(1)} %copy-done, bf16[1280,192]{0,1:T(8,128)(2,1)S(1)} %copy.37, pred[]{:T(512)} %get-tuple-element.36), kind=kLoop, calls=%fused_computation.30 | loop fusion | flops 2457599 | bytes 1966085 | tf_op jit(solution)/shard_map/reduce_sum | solution.py:61
  57.7 1.5 %convolution_convert_fusion.5 = bf16[192,192]{1,0:T(8,128)(2,1)S(1)} fusion(bf16[192,1280]{1,0:T(8,128)(2,1)} %get-tuple-element.43, f32[]{:T(128)S(6)} %add.75), kind=kOutput, calls=%fused_computation.29 | convolution fusion | flops 95145984 | bytes 565252 | tf_op jit(solution)/shard_map/dot_general | solution.py:66
  59.2 1.6 %fusion.3 = bf16[1280,192]{0,1:T(8,128)(2,1)S(1)} fusion(bf16[192,192]{1,0:T(8,128)(2,1)S(1)} %convolution_convert_fusion.5, f32[]{:T(128)S(6)} %add.75, bf16[192,1280]{1,0:T(8,128)(2,1)} %get-tuple-element.43), kind=kOutput, calls=%fused_computation.9 | convolution fusion | flops 111169536 | bytes 1056772 | tf_op jit(solution)/shard_map/dot_general | solution.py:80
  61.1 1.0 collective-permute-done
  62.2 1.6 %collective-permute-done.1 = bf16[1280,192]{0,1:T(8,128)(2,1)S(1)} collective-permute-done((bf16[1280,192]{0,1:T(8,128)(2,1)}, bf16[1280,192]{0,1:T(8,128)(2,1)S(1)}, u32[]{:S(2)}, u32[]{:S(2)}) %collective-permute-start.1) | collective-permute-done | bytes 491552 | tf_op jit(solution)/shard_map/ppermute | solution.py:107
  64.5 3.1 %collective-permute-start.2 = (bf16[1280,96]{0,1:T(8,128)(2,1)}, bf16[1280,96]{0,1:T(8,128)(2,1)}, u32[]{:S(2)}, u32[]{:S(2)}) collective-permute-start(bf16[1280,96]{0,1:T(8,128)(2,1)} %slice.30), channel_id=1, source_target_pairs={{0,1},{1,2},{2,3},{3,0},{4,5},{5,6},{6,7},{7,4},{8,9},{9,10},{10,1... | collective-permute-start | bytes 737288 | tf_op jit(solution)/shard_map/ppermute | solution.py:110
  67.6 1.2 fusion.4
  68.9 3.4 %collective-permute-start.3 = (bf16[1280,96]{0,1:T(8,128)(2,1)S(1)}, bf16[1280,96]{0,1:T(8,128)(2,1)S(1)}, u32[]{:S(2)}, u32[]{:S(2)}) collective-permute-start(bf16[1280,96]{0,1:T(8,128)(2,1)S(1)} %slice.31), channel_id=1, source_target_pairs={{0,3},{1,0},{2,1},{3,2},{4,7},{5,4},{6,5},{7,6},{8,11},{9,8},{10,9... | collective-permute-start | bytes 737288 | tf_op jit(solution)/shard_map/ppermute | solution.py:111
  73.1 0.9 copy.43
  74.0 9.7 %all-to-all-start.2 = ((f32[128,1,336]{2,1,0:T(1,128)}), f32[128,1,336]{2,1,0:T(1,128)S(1)}, u32[]{:S(2)}, u32[]{:S(2)}) async-start(f32[128,1,336]{2,1,0:T(1,128)} %copy.43), calls=%async_computation.2 | async-start | bytes 393216 | tf_op jit(solution)/shard_map/all_to_all | solution.py:156
  83.7 1.7 %constant_dynamic-update-slice_fusion.2 = bf16[1280,768]{0,1:T(8,128)(2,1)} fusion(bf16[1280,768]{0,1:T(8,128)(2,1)} %constant_dynamic-update-slice_fusion.3, bf16[1280,96]{0,1:T(8,128)(2,1)} %collective-permute-done.2), kind=kLoop, calls=%fused_computation.81 | loop fusion | bytes 491520
  86.1 0.8 constant_dynamic-update-slice_fusion
  86.9 3.2 %fusion = f32[]{:T(128)} fusion(bf16[1280,768]{0,1:T(8,128)(2,1)} %constant_dynamic-update-slice_fusion), kind=kLoop, calls=%fused_computation.2 | loop fusion | flops 2949119 | bytes 1966084 | tf_op jit(solution)/shard_map/reduce_sum | solution.py:61
  90.8 3.9 %convolution_convert_fusion.3 = bf16[768,768]{1,0:T(8,128)(2,1)S(1)} fusion(bf16[1280,768]{0,1:T(8,128)(2,1)} %constant_dynamic-update-slice_fusion, f32[]{:T(128)S(6)} %add.68), kind=kOutput, calls=%fused_computation.16 | convolution fusion | flops 1513488384 | bytes 3145732 | tf_op jit(solution)/shard_map/dot_general | solution.py:66
  94.7 6.2 %add_convert_fusion = bf16[1280,768]{0,1:T(8,128)(2,1)} fusion(bf16[768,768]{1,0:T(8,128)(2,1)S(1)} %convolution_convert_fusion.3, f32[]{:T(128)S(6)} %add.68, bf16[1280,768]{0,1:T(8,128)(2,1)} %constant_dynamic-update-slice_fusion), kind=kOutput, calls=%fused_computation.4 | convolution fusion | flops 2428698624 | bytes 5111812 | tf_op jit(solution)/shard_map/dot_general | solution.py:80
  100.9 4.9 %convolution_convert_fusion.2 = bf16[768,768]{1,0:T(8,128)(2,1)} fusion(bf16[1280,768]{0,1:T(8,128)(2,1)} %add_convert_fusion), kind=kOutput, calls=%fused_computation.15 | convolution fusion | flops 1510539264 | bytes 3145728 | tf_op jit(solution)/shard_map/dot_general | solution.py:66
  105.8 3.7 %fusion.5 = bf16[1280,192]{0,1:T(8,128)(2,1)S(1)} fusion(bf16[1280,192]{0,1:T(8,128)(2,1)S(1)} %copy-done.9, bf16[1280,768]{0,1:T(8,128)(2,1)} %add_convert_fusion, bf16[768,768]{1,0:T(8,128)(2,1)} %convolution_convert_fusion.2, pred[]{:T(512)} %get-tuple-element.35), kind=kOutput, calls=%fused_computation.11 | convolution fusion | flops 605945856 | bytes 5210624 | tf_op jit(solution)/shard_map/dot_general | solution.py:80
  110.1 1.6 %reshape.57 = bf16[128,2,960]{2,1,0:T(2,128)(2,1)} reshape(bf16[128,10,192]{2,1,0:T(8,128)(2,1)S(1)} %reshape.44) | data formatting | bytes 983040
  111.6 13.9 %all-to-all-start.1 = ((bf16[128,2,960]{2,1,0:T(2,128)(2,1)}), bf16[128,2,960]{2,1,0:T(2,128)(2,1)S(1)}, u32[]{:S(2)}, u32[]{:S(2)}) async-start(bf16[128,2,960]{2,1,0:T(2,128)(2,1)} %reshape.57), calls=%async_computation.1 | async-start | bytes 1048576 | tf_op jit(solution)/shard_map/all_to_all | solution.py:166
  125.5 1.0 copy.42
  126.5 1.0 copy.40
  127.6 4.0 %fusion.15 = (f32[1,192,1280]{2,1,0:T(8,128)}, f32[1,192,1280]{2,1,0:T(8,128)}) fusion(f32[192,1280]{1,0:T(8,128)S(1)} %bitcast.78, bf16[1280,192]{0,1:T(8,128)(2,1)} %copy.42, pred[]{:T(512)} %get-tuple-element.36, f32[192,1280]{1,0:T(8,128)S(1)} %bitcast.79, bf16[1280,192]{0,1:T(8,128)(2,1)} %copy.40, pred[]{:T(512)} %get-tuple-element.35), kind=kLoop, calls=%fused_computation.34 | loop fusion | flops 1966080 | bytes 4915202 | tf_op jit(solution)/shard_map/broadcast_in_dim | solution.py:185
  132.4 12.5 %all-to-all-done.1 = bf16[128,2,960]{2,1,0:T(2,128)(2,1)S(1)} async-done(((bf16[128,2,960]{2,1,0:T(2,128)(2,1)}), bf16[128,2,960]{2,1,0:T(2,128)(2,1)S(1)}, u32[]{:S(2)}, u32[]{:S(2)}) %all-to-all-start.1) | async-done | bytes 491552 | tf_op jit(solution)/shard_map/all_to_all | solution.py:166
  (54 shorter events, 11.8 us)
Async XLA Ops:
  0.6 1.6 %copy-start.5 = (s32[2,32]{1,0:T(2,128)S(1)}, s32[2,32]{1,0:T(2,128)}, u32[]{:S(2)}) copy-start(s32[2,32]{1,0:T(2,128)} %param.17) | copy-start | bytes 772
  2.9 21.9 %copy-start.2 = (f32[1,43008]{1,0:T(1,128)S(1)}, f32[1,43008]{1,0:T(1,128)}, u32[]{:S(2)}) copy-start(f32[1,43008]{1,0:T(1,128)} %param.18) | copy-start | bytes 516100
  5.8 37.8 %all-to-all-start = ((bf16[128,2,960]{2,1,0:T(2,128)(2,1)}), bf16[128,2,960]{2,1,0:T(2,128)(2,1)S(1)}, u32[]{:S(2)}, u32[]{:S(2)}) async-start(bf16[128,2,960]{2,1,0:T(2,128)(2,1)} %reshape.55), calls=%async_computation | async-start | bytes 1048576 | tf_op jit(solution)/shard_map/all_to_all | solution.py:143
  44.9 9.8 %copy-start = (f32[1,192,1280]{2,1,0:T(8,128)S(1)}, f32[1,192,1280]{2,1,0:T(8,128)}, u32[]{:S(2)}) copy-start(f32[1,192,1280]{2,1,0:T(8,128)} %param.16) | copy-start | bytes 2949124
  48.2 14.0 %collective-permute-start = (bf16[1280,192]{0,1:T(8,128)(2,1)}, bf16[1280,192]{0,1:T(8,128)(2,1)S(1)}, u32[]{:S(2)}, u32[]{:S(2)}) collective-permute-start(bf16[1280,192]{0,1:T(8,128)(2,1)} %get-tuple-element.41), channel_id=1, source_target_pairs={{0,1},{1,2},{2,3},{3,0},{4,5},{5,6},{6,7},{7,4},{8,9},{9,10},{10,1... | collective-permute-start | bytes 1474568 | tf_op jit(solution)/shard_map/ppermute | solution.py:106
  51.3 12.5 %collective-permute-start.1 = (bf16[1280,192]{0,1:T(8,128)(2,1)}, bf16[1280,192]{0,1:T(8,128)(2,1)S(1)}, u32[]{:S(2)}, u32[]{:S(2)}) collective-permute-start(bf16[1280,192]{0,1:T(8,128)(2,1)} %get-tuple-element.41), channel_id=1, source_target_pairs={{0,3},{1,0},{2,1},{3,2},{4,7},{5,4},{6,5},{7,6},{8,11},{9,8},{10,9... | collective-permute-start | bytes 1474568 | tf_op jit(solution)/shard_map/ppermute | solution.py:107
  64.5 19.2 %collective-permute-start.2 = (bf16[1280,96]{0,1:T(8,128)(2,1)}, bf16[1280,96]{0,1:T(8,128)(2,1)}, u32[]{:S(2)}, u32[]{:S(2)}) collective-permute-start(bf16[1280,96]{0,1:T(8,128)(2,1)} %slice.30), channel_id=1, source_target_pairs={{0,1},{1,2},{2,3},{3,0},{4,5},{5,6},{6,7},{7,4},{8,9},{9,10},{10,1... | collective-permute-start | bytes 737288 | tf_op jit(solution)/shard_map/ppermute | solution.py:110
  68.9 16.5 %collective-permute-start.3 = (bf16[1280,96]{0,1:T(8,128)(2,1)S(1)}, bf16[1280,96]{0,1:T(8,128)(2,1)S(1)}, u32[]{:S(2)}, u32[]{:S(2)}) collective-permute-start(bf16[1280,96]{0,1:T(8,128)(2,1)S(1)} %slice.31), channel_id=1, source_target_pairs={{0,3},{1,0},{2,1},{3,2},{4,7},{5,4},{6,5},{7,6},{8,11},{9,8},{10,9... | collective-permute-start | bytes 737288 | tf_op jit(solution)/shard_map/ppermute | solution.py:111
  74.0 37.7 %all-to-all-start.2 = ((f32[128,1,336]{2,1,0:T(1,128)}), f32[128,1,336]{2,1,0:T(1,128)S(1)}, u32[]{:S(2)}, u32[]{:S(2)}) async-start(f32[128,1,336]{2,1,0:T(1,128)} %copy.43), calls=%async_computation.2 | async-start | bytes 393216 | tf_op jit(solution)/shard_map/all_to_all | solution.py:156
  100.9 4.9 %copy-start.9 = (bf16[1280,192]{0,1:T(8,128)(2,1)S(1)}, bf16[1280,192]{0,1:T(8,128)(2,1)}, u32[]{:S(2)}) copy-start(bf16[1280,192]{0,1:T(8,128)(2,1)} %fusion.4) | copy-start | bytes 1474564
  111.6 15.9 %copy-start.1 = (f32[1,192,1280]{2,1,0:T(8,128)S(1)}, f32[1,192,1280]{2,1,0:T(8,128)}, u32[]{:S(2)}) copy-start(f32[1,192,1280]{2,1,0:T(8,128)} %param.13) | copy-start | bytes 2949124
  111.6 33.3 %all-to-all-start.1 = ((bf16[128,2,960]{2,1,0:T(2,128)(2,1)}), bf16[128,2,960]{2,1,0:T(2,128)(2,1)S(1)}, u32[]{:S(2)}, u32[]{:S(2)}) async-start(bf16[128,2,960]{2,1,0:T(2,128)(2,1)} %reshape.57), calls=%async_computation.1 | async-start | bytes 1048576 | tf_op jit(solution)/shard_map/all_to_all | solution.py:166
  127.5 4.2 %copy-start.6 = (f32[336]{0:T(512)S(1)}, f32[336]{0:T(512)}, u32[]{:S(2)}) copy-start(f32[336]{0:T(512)} %param.19) | copy-start | bytes 4036
  127.5 4.2 %copy-start.7 = (f32[336]{0:T(512)S(1)}, f32[336]{0:T(512)}, u32[]{:S(2)}) copy-start(f32[336]{0:T(512)} %param.20) | copy-start | bytes 4036
  127.5 4.2 %copy-start.8 = (f32[336]{0:T(512)S(1)}, f32[336]{0:T(512)}, u32[]{:S(2)}) copy-start(f32[336]{0:T(512)} %param.21) | copy-start | bytes 4036
  145.7 1.3 copy-start.3
  146.8 1.3 copy-start.4

commit v6 on v4

--- a/solution.py
+++ b/solution.py
@@ -94,20 +94,19 @@
     ).astype(jnp.bfloat16)
 
 
-def gather_columns(column_part, rider):
+def gather_columns(column_part):
     count = lax.axis_size("tensor")
     ahead = [(i, (i + 1) % count) for i in range(count)]
     behind = [(i, (i - 1) % count) for i in range(count)]
     from_behind = lax.ppermute(column_part, "tensor", ahead)
     from_ahead = lax.ppermute(column_part, "tensor", behind)
-    from_behind, from_ahead, rider = lax.optimization_barrier((from_behind, from_ahead, rider))
     half = column_part.shape[1] // 2
     far_first = lax.ppermute(from_behind[:, :half], "tensor", ahead)
     far_second = lax.ppermute(from_ahead[:, half:], "tensor", behind)
     gathered = jnp.concatenate(
         [column_part, from_behind, far_first, far_second, from_ahead], axis=1
     )
-    return gathered, rider
+    return gathered
 
 
 def gather_gram(gram_part):
@@ -135,19 +134,19 @@
     matrices = big_grad.shape[0]
     joint_map = owner_table(jnp.concatenate([owners[0], owners[1]]), shards)
     joint_pieces = jnp.concatenate([big_grad, small_grad], axis=0)
-    arrived = lax.all_to_all(
-        route_rows(joint_map, joint_pieces), "shard", split_axis=0, concat_axis=1, tiled=True
-    )[0]
+    routed = route_rows(joint_map, joint_pieces).reshape(shards, -1)
+    outgoing = jnp.concatenate(
+        [routed, vec_parts[0].astype(jnp.bfloat16).reshape(shards, -1)], axis=1
+    )
+    incoming = lax.all_to_all(outgoing, "shard", split_axis=0, concat_axis=0, tiled=True)
+    arrived = incoming[:, : routed.shape[1]].reshape(shards * rows_dev, block_width)
+    grad_share = jnp.sum(incoming[:, routed.shape[1] :].astype(jnp.float32), axis=0)
     big_owner = jnp.any(owners[0] == shard_place)
     small_owner = jnp.any(owners[1] == shard_place)
     big_retained, big_blended = advance(arrived, big_moment[0], big_owner)
     small_retained, small_blended = advance(arrived, small_moment[0], small_owner)
     small_result = small_newton(small_blended)
-    gathered, vec_pieces = gather_columns(big_blended, vec_parts[0].reshape(shards, -1))
-    full_iterate = normalized(gathered)
-    grad_share = jnp.sum(
-        lax.all_to_all(vec_pieces, "shard", split_axis=0, concat_axis=0, tiled=True), axis=0
-    )
+    full_iterate = normalized(gather_columns(big_blended))
     for iteration in range(ITERS - 1):
         gram_full = gram_block(full_iterate, full_iterate)
         full_iterate = newton_step(full_iterate, full_iterate, poly_block(gram_full, gram_full))

time: 143 us -> 136 us (0.951); the launches traced: 143 us -> 134 us
  starting transfers between devices: 54.9 us -> 42.3 us
  waiting for transfers between devices: 39.5 us -> 42.1 us
    all_to_all x2 -> x1, starting transfers between devices: 28.1 us -> 18.4 us  [per_device(): lax.all_to_all(outgoing, 'shard', split_axis=0, concat_axis=0, tiled=True)]
    all_to_all x2 -> x1, waiting for transfers between devices: 17 us -> 20.2 us  [per_device(): lax.all_to_all(outgoing, 'shard', split_axis=0, concat_axis=0, tiled=True)]
    all_to_all x1, starting transfers between devices: 13.7 us -> 10.7 us  [per_device(): lax.all_to_all(own_result.reshape(shards, rows_dev, block_width), 'shard'...]
    ppermute x1, waiting for transfers between devices: 0.01 us -> 1.83 us  [gather_columns(): far_second = lax.ppermute(from_ahead[:, half:], 'tensor', behind)]
    ppermute x1, waiting for transfers between devices: 1.64 us -> 0.01 us  [gather_columns(): from_ahead = lax.ppermute(column_part, 'tensor', behind)]
    unnamed x34 -> x35, local copies, waits for them, and re-layouts: 8.6 us -> 8.26 us
  transfers between devices with their start and end apart: 7 -> 6, of which waited for: 4 -> 4; matrix products, arithmetic and copies ran while one was open for 22% -> 8% of each run, Pallas kernels for 0% -> 0%
where the time goes in v6:
time: 136 us; the launch traced here: 134 us
  starting transfers between devices  42.3 us (31%)
  waiting for transfers between devices  42.1 us (31%)
  local copies, waits for them, and re-layouts  17.6 us (13%)
  matrix products  16.9 us (12%)
  other arithmetic  12.3 us (9%)
  between operations  2.45 us (2%)
    all_to_all x1, waiting for transfers between devices, per_device(): lax.all_to_all(outgoing, 'shard', split_axis=0, concat_axis=0, tiled=True)  20.2 us
    all_to_all x1, starting transfers between devices, per_device(): lax.all_to_all(outgoing, 'shard', split_axis=0, concat_axis=0, tiled=True)  18.4 us
    all_to_all x1, waiting for transfers between devices, per_device(): lax.all_to_all(own_result.reshape(shards, rows_dev, block_width), 'shard'...  17.8 us
    all_to_all x1, starting transfers between devices, per_device(): lax.all_to_all(own_result.reshape(shards, rows_dev, block_width), 'shard'...  10.7 us
    dot_general x4, matrix products, newton_step(): lax.dot_general(full_iterate, polynomial, (((1,), (1,)), ((), ())), prefe...  8.88 us
    unnamed x35, local copies, waits for them, and re-layouts  8.26 us
    dot_general x4, matrix products, gram_block(): lax.dot_general(left_part, right_part, (((0,), (0,)), ((), ())), preferre...  7.43 us
    reduce_sum x2, other arithmetic, normalized(): squares = jnp.sum(values * values)  5.19 us
  transfers between devices with their start and end apart: 6, of which 4 were waited for; matrix products, arithmetic and copies ran while one was open for 8% of the time, Pallas kernels for 0%

profile of v6, /device:TPU:1, one launch (start us, length us, event | category | flops | bytes accessed | tf_op | source)
XLA Modules:
  0.0 133.6 jit_solution(3317872000324511465)
XLA Ops:
  0.6 0.8 slice_bitcast_fusion.1
  1.4 1.0 pad_maximum_fusion
  4.6 1.0 reduce.3
  5.6 1.4 %reshape.46 = bf16[128,2,1128]{2,1,0:T(2,128)(2,1)} reshape(bf16[128,2256]{1,0:T(8,128)(2,1)S(1)} %reduce.3) | data formatting | bytes 1155072
  7.1 18.4 %all-to-all-start = ((bf16[128,2,1128]{2,1,0:T(2,128)(2,1)}), bf16[128,2,1128]{2,1,0:T(2,128)(2,1)S(1)}, u32[]{:S(2)}, u32[]{:S(2)}) async-start(bf16[128,2,1128]{2,1,0:T(2,128)(2,1)} %reshape.46), calls=%async_computation | async-start | bytes 1179648 | tf_op jit(solution)/shard_map/all_to_all | solution.py:141
  26.1 20.2 %all-to-all-done = bf16[128,2,1128]{2,1,0:T(2,128)(2,1)S(1)} async-done(((bf16[128,2,1128]{2,1,0:T(2,128)(2,1)}), bf16[128,2,1128]{2,1,0:T(2,128)(2,1)S(1)}, u32[]{:S(2)}, u32[]{:S(2)}) %all-to-all-start) | async-done | bytes 577568 | tf_op jit(solution)/shard_map/all_to_all | solution.py:141
  46.3 0.9 reshape.47
  47.2 1.6 %copy.41 = bf16[128,1,2256]{0,2,1:T(8,128)(2,1)S(1)} copy(bf16[128,1,2256]{2,1,0:T(2,128)(2,1)S(1)} %reshape.47) | data formatting | bytes 1155072 | tf_op jit(solution)/shard_map/all_to_all | solution.py:141
  51.2 1.8 %constant_dynamic-update-slice_fusion.4 = (bf16[1280,768]{0,1:T(8,128)(2,1)}, bf16[1280,192]{0,1:T(8,128)(2,1)}) fusion(f32[1,192,1280]{2,1,0:T(8,128)S(1)} %copy-done, f32[1280,192]{0,1:T(8,128)S(1)} %copy.43, pred[]{:T(512)} %get-tuple-element.28), kind=kLoop, calls=%fused_computation.85 | loop fusion | flops 1474559 | bytes 2949121
  53.0 3.1 %collective-permute-start = (bf16[1280,192]{0,1:T(8,128)(2,1)}, bf16[1280,192]{0,1:T(8,128)(2,1)}, u32[]{:S(2)}, u32[]{:S(2)}) collective-permute-start(bf16[1280,192]{0,1:T(8,128)(2,1)} %get-tuple-element.34), channel_id=1, source_target_pairs={{0,1},{1,2},{2,3},{3,0},{4,5},{5,6},{6,7},{7,4},{8,9},{9,10},{10,1... | collective-permute-start | bytes 1474568 | tf_op jit(solution)/shard_map/ppermute | solution.py:101
  56.1 3.4 %collective-permute-start.2 = (bf16[1280,192]{0,1:T(8,128)(2,1)}, bf16[1280,192]{0,1:T(8,128)(2,1)}, u32[]{:S(2)}, u32[]{:S(2)}) collective-permute-start(bf16[1280,192]{0,1:T(8,128)(2,1)} %get-tuple-element.34), channel_id=1, source_target_pairs={{0,3},{1,0},{2,1},{3,2},{4,7},{5,4},{6,5},{7,6},{8,11},{9,8},{10,9... | collective-permute-start | bytes 1474568 | tf_op jit(solution)/shard_map/ppermute | solution.py:102
  59.5 3.6 %fusion.12 = (f32[]{:T(128)}, bf16[192,1280]{1,0:T(8,128)(2,1)S(1)}, f32[1,192,1280]{2,1,0:T(8,128)}, f32[1,192,1280]{2,1,0:T(8,128)}) fusion(f32[1,192,1280]{2,1,0:T(8,128)S(1)} %copy-done.3, f32[1280,192]{0,1:T(8,128)S(1)} %copy.43, pred[]{:T(512)} %get-tuple-element.29, f32[1,192,1280]{2,1,0:T(8,128)S(1)} %copy-done, pred[]{:T(512)} %get-tuple-element.28), kind=kLoop, calls=%fused_computation.30 | loop fusion | flops 3194879 | bytes 5406726 | tf_op jit(solution)/shard_map/reduce_sum | solution.py:56
  64.9 2.2 %collective-permute-done = bf16[1280,192]{0,1:T(8,128)(2,1)} collective-permute-done((bf16[1280,192]{0,1:T(8,128)(2,1)}, bf16[1280,192]{0,1:T(8,128)(2,1)}, u32[]{:S(2)}, u32[]{:S(2)}) %collective-permute-start) | collective-permute-done | bytes 491552 | tf_op jit(solution)/shard_map/ppermute | solution.py:101
  67.1 1.0 slice.45
  68.1 1.9 %collective-permute-start.1 = (bf16[1280,96]{0,1:T(8,128)(2,1)S(1)}, bf16[1280,96]{0,1:T(8,128)(2,1)S(1)}, u32[]{:S(2)}, u32[]{:S(2)}) collective-permute-start(bf16[1280,96]{0,1:T(8,128)(2,1)S(1)} %slice.45), channel_id=1, source_target_pairs={{0,1},{1,2},{2,3},{3,0},{4,5},{5,6},{6,7},{7,4},{8,9},{9,10},{10,1... | collective-permute-start | bytes 737288 | tf_op jit(solution)/shard_map/ppermute | solution.py:104
  70.0 1.2 fusion.4
  71.3 1.0 slice.46
  72.2 4.8 %collective-permute-start.3 = (bf16[1280,96]{0,1:T(8,128)(2,1)S(1)}, bf16[1280,96]{0,1:T(8,128)(2,1)S(1)}, u32[]{:S(2)}, u32[]{:S(2)}) collective-permute-start(bf16[1280,96]{0,1:T(8,128)(2,1)S(1)} %slice.46), channel_id=1, source_target_pairs={{0,3},{1,0},{2,1},{3,2},{4,7},{5,4},{6,5},{7,6},{8,11},{9,8},{10,9... | collective-permute-start | bytes 737288 | tf_op jit(solution)/shard_map/ppermute | solution.py:105
  77.0 1.1 constant_dynamic-update-slice_fusion.3
  78.1 1.8 %collective-permute-done.3 = bf16[1280,96]{0,1:T(8,128)(2,1)S(1)} collective-permute-done((bf16[1280,96]{0,1:T(8,128)(2,1)S(1)}, bf16[1280,96]{0,1:T(8,128)(2,1)S(1)}, u32[]{:S(2)}, u32[]{:S(2)}) %collective-permute-start.3) | collective-permute-done | bytes 245792 | tf_op jit(solution)/shard_map/ppermute | solution.py:105
  79.9 1.1 constant_dynamic-update-slice_fusion
  81.0 1.6 %fusion = f32[]{:T(128)} fusion(bf16[1280,768]{0,1:T(8,128)(2,1)S(1)} %constant_dynamic-update-slice_fusion), kind=kLoop, calls=%fused_computation.2 | loop fusion | flops 2949119 | bytes 1966084 | tf_op jit(solution)/shard_map/reduce_sum | solution.py:56
  83.3 1.8 %convolution_convert_fusion.3 = bf16[768,768]{1,0:T(8,128)(2,1)S(1)} fusion(bf16[1280,768]{0,1:T(8,128)(2,1)S(1)} %constant_dynamic-update-slice_fusion, f32[]{:T(128)S(6)} %add.62), kind=kOutput, calls=%fused_computation.16 | convolution fusion | flops 1513488384 | bytes 3145732 | tf_op jit(solution)/shard_map/dot_general | solution.py:61
  85.1 4.2 %add_convert_fusion = bf16[1280,768]{0,1:T(8,128)(2,1)} fusion(bf16[768,768]{1,0:T(8,128)(2,1)S(1)} %convolution_convert_fusion.3, f32[]{:T(128)S(6)} %add.62, bf16[1280,768]{0,1:T(8,128)(2,1)S(1)} %constant_dynamic-update-slice_fusion), kind=kOutput, calls=%fused_computation.4 | convolution fusion | flops 2428698624 | bytes 5111812 | tf_op jit(solution)/shard_map/dot_general | solution.py:75
  89.3 5.0 %convolution_convert_fusion.2 = bf16[768,768]{1,0:T(8,128)(2,1)} fusion(bf16[1280,768]{0,1:T(8,128)(2,1)} %add_convert_fusion), kind=kOutput, calls=%fused_computation.15 | convolution fusion | flops 1510539264 | bytes 3145728 | tf_op jit(solution)/shard_map/dot_general | solution.py:61
  94.3 3.0 %fusion.5 = bf16[1280,192]{0,1:T(8,128)(2,1)S(1)} fusion(bf16[1280,192]{0,1:T(8,128)(2,1)S(1)} %copy-done.11, bf16[1280,768]{0,1:T(8,128)(2,1)S(1)} %copy-done.12, bf16[768,768]{1,0:T(8,128)(2,1)} %convolution_convert_fusion.2, pred[]{:T(512)} %get-tuple-element.28), kind=kOutput, calls=%fused_computation.11 | convolution fusion | flops 605945856 | bytes 5210624 | tf_op jit(solution)/shard_map/dot_general | solution.py:75
  97.9 1.5 %reshape.48 = bf16[128,2,960]{2,1,0:T(2,128)(2,1)} reshape(bf16[128,10,192]{2,1,0:T(8,128)(2,1)S(1)} %reshape.42) | data formatting | bytes 983040
  99.4 10.7 %all-to-all-start.1 = ((bf16[128,2,960]{2,1,0:T(2,128)(2,1)}), bf16[128,2,960]{2,1,0:T(2,128)(2,1)S(1)}, u32[]{:S(2)}, u32[]{:S(2)}) async-start(bf16[128,2,960]{2,1,0:T(2,128)(2,1)} %reshape.48), calls=%async_computation.1 | async-start | bytes 1048576 | tf_op jit(solution)/shard_map/all_to_all | solution.py:158
  110.1 1.0 convert_reduce_fusion
  111.8 17.8 %all-to-all-done.1 = bf16[128,2,960]{2,1,0:T(2,128)(2,1)S(1)} async-done(((bf16[128,2,960]{2,1,0:T(2,128)(2,1)}), bf16[128,2,960]{2,1,0:T(2,128)(2,1)S(1)}, u32[]{:S(2)}, u32[]{:S(2)}) %all-to-all-start.1) | async-done | bytes 491552 | tf_op jit(solution)/shard_map/all_to_all | solution.py:158
  129.6 0.8 reshape.49
  130.3 0.7 copy.45
  (57 shorter events, 9.8 us)
Async XLA Ops:
  0.6 2.4 %copy-start.4 = (f32[1,43008]{1,0:T(1,128)S(1)}, f32[1,43008]{1,0:T(1,128)}, u32[]{:S(2)}) copy-start(f32[1,43008]{1,0:T(1,128)} %param.18) | copy-start | bytes 516100
  4.1 21.4 %copy-start.7 = (s32[2,32]{1,0:T(2,128)S(1)}, s32[2,32]{1,0:T(2,128)}, u32[]{:S(2)}) copy-start(s32[2,32]{1,0:T(2,128)} %param.17) | copy-start | bytes 772
  7.1 39.3 %all-to-all-start = ((bf16[128,2,1128]{2,1,0:T(2,128)(2,1)}), bf16[128,2,1128]{2,1,0:T(2,128)(2,1)S(1)}, u32[]{:S(2)}, u32[]{:S(2)}) async-start(bf16[128,2,1128]{2,1,0:T(2,128)(2,1)} %reshape.46), calls=%async_computation | async-start | bytes 1179648 | tf_op jit(solution)/shard_map/all_to_all | solution.py:141
  48.8 0.8 copy-start.2
  50.0 1.2 copy-start
  50.9 8.6 %copy-start.3 = (f32[1,192,1280]{2,1,0:T(8,128)S(1)}, f32[1,192,1280]{2,1,0:T(8,128)}, u32[]{:S(2)}) copy-start(f32[1,192,1280]{2,1,0:T(8,128)} %param.16) | copy-start | bytes 2949124
  53.0 14.1 %collective-permute-start = (bf16[1280,192]{0,1:T(8,128)(2,1)}, bf16[1280,192]{0,1:T(8,128)(2,1)}, u32[]{:S(2)}, u32[]{:S(2)}) collective-permute-start(bf16[1280,192]{0,1:T(8,128)(2,1)} %get-tuple-element.34), channel_id=1, source_target_pairs={{0,1},{1,2},{2,3},{3,0},{4,5},{5,6},{6,7},{7,4},{8,9},{9,10},{10,1... | collective-permute-start | bytes 1474568 | tf_op jit(solution)/shard_map/ppermute | solution.py:101
  56.1 15.1 %collective-permute-start.2 = (bf16[1280,192]{0,1:T(8,128)(2,1)}, bf16[1280,192]{0,1:T(8,128)(2,1)}, u32[]{:S(2)}, u32[]{:S(2)}) collective-permute-start(bf16[1280,192]{0,1:T(8,128)(2,1)} %get-tuple-element.34), channel_id=1, source_target_pairs={{0,3},{1,0},{2,1},{3,2},{4,7},{5,4},{6,5},{7,6},{8,11},{9,8},{10,9... | collective-permute-start | bytes 1474568 | tf_op jit(solution)/shard_map/ppermute | solution.py:102
  64.6 12.4 %copy-start.1 = (bf16[1280,768]{0,1:T(8,128)(2,1)S(1)}, bf16[1280,768]{0,1:T(8,128)(2,1)}, u32[]{:S(2)}) copy-start(bf16[1280,768]{0,1:T(8,128)(2,1)} %get-tuple-element.33) | copy-start | bytes 5898244
  68.1 10.0 %collective-permute-start.1 = (bf16[1280,96]{0,1:T(8,128)(2,1)S(1)}, bf16[1280,96]{0,1:T(8,128)(2,1)S(1)}, u32[]{:S(2)}, u32[]{:S(2)}) collective-permute-start(bf16[1280,96]{0,1:T(8,128)(2,1)S(1)} %slice.45), channel_id=1, source_target_pairs={{0,1},{1,2},{2,3},{3,0},{4,5},{5,6},{6,7},{7,4},{8,9},{9,10},{10,1... | collective-permute-start | bytes 737288 | tf_op jit(solution)/shard_map/ppermute | solution.py:104
  72.2 7.7 %collective-permute-start.3 = (bf16[1280,96]{0,1:T(8,128)(2,1)S(1)}, bf16[1280,96]{0,1:T(8,128)(2,1)S(1)}, u32[]{:S(2)}, u32[]{:S(2)}) collective-permute-start(bf16[1280,96]{0,1:T(8,128)(2,1)S(1)} %slice.46), channel_id=1, source_target_pairs={{0,3},{1,0},{2,1},{3,2},{4,7},{5,4},{6,5},{7,6},{8,11},{9,8},{10,9... | collective-permute-start | bytes 737288 | tf_op jit(solution)/shard_map/ppermute | solution.py:105
  89.3 5.0 %copy-start.11 = (bf16[1280,192]{0,1:T(8,128)(2,1)S(1)}, bf16[1280,192]{0,1:T(8,128)(2,1)}, u32[]{:S(2)}) copy-start(bf16[1280,192]{0,1:T(8,128)(2,1)} %fusion.4) | copy-start | bytes 1474564
  89.3 5.0 %copy-start.12 = (bf16[1280,768]{0,1:T(8,128)(2,1)S(1)}, bf16[1280,768]{0,1:T(8,128)(2,1)}, u32[]{:S(2)}) copy-start(bf16[1280,768]{0,1:T(8,128)(2,1)} %add_convert_fusion) | copy-start | bytes 5898244
  97.6 13.6 %copy-start.8 = (f32[336]{0:T(512)S(1)}, f32[336]{0:T(512)}, u32[]{:S(2)}) copy-start(f32[336]{0:T(512)} %param.19) | copy-start | bytes 4036
  97.6 13.6 %copy-start.9 = (f32[336]{0:T(512)S(1)}, f32[336]{0:T(512)}, u32[]{:S(2)}) copy-start(f32[336]{0:T(512)} %param.20) | copy-start | bytes 4036
  97.6 13.6 %copy-start.10 = (f32[336]{0:T(512)S(1)}, f32[336]{0:T(512)}, u32[]{:S(2)}) copy-start(f32[336]{0:T(512)} %param.21) | copy-start | bytes 4036
  99.4 30.1 %all-to-all-start.1 = ((bf16[128,2,960]{2,1,0:T(2,128)(2,1)}), bf16[128,2,960]{2,1,0:T(2,128)(2,1)S(1)}, u32[]{:S(2)}, u32[]{:S(2)}) async-start(bf16[128,2,960]{2,1,0:T(2,128)(2,1)} %reshape.48), calls=%async_computation.1 | async-start | bytes 1048576 | tf_op jit(solution)/shard_map/all_to_all | solution.py:158
  130.3 1.3 copy-start.5
  131.4 1.3 copy-start.6

commit v7 on v6

--- a/solution.py
+++ b/solution.py
@@ -132,9 +132,16 @@
     block_width = big_grad.shape[2]
     rows_dev = big_grad.shape[1]
     matrices = big_grad.shape[0]
-    joint_map = owner_table(jnp.concatenate([owners[0], owners[1]]), shards)
+    owner_list = jnp.concatenate([owners[0], owners[1]])
+    joint_map = owner_table(owner_list, shards)
     joint_pieces = jnp.concatenate([big_grad, small_grad], axis=0)
-    routed = route_rows(joint_map, joint_pieces).reshape(shards, -1)
+    listed = lax.broadcasted_iota(jnp.int32, (shards, owner_list.shape[0]), 1)
+    hits = lax.broadcasted_iota(jnp.int32, (shards, owner_list.shape[0]), 0) == owner_list[None, :]
+    owned_index = jnp.sum(jnp.where(hits, listed, 0), axis=1) + jnp.where(
+        jnp.any(hits, axis=1), 0, owner_list.shape[0]
+    )
+    padded_pieces = jnp.concatenate([joint_pieces, jnp.zeros_like(joint_pieces[:1])], axis=0)
+    routed = jnp.take(padded_pieces, owned_index, axis=0).reshape(shards, -1)
     outgoing = jnp.concatenate(
         [routed, vec_parts[0].astype(jnp.bfloat16).reshape(shards, -1)], axis=1
     )
@@ -162,7 +169,7 @@
         concat_axis=0,
         tiled=True,
     )
-    picked = collect(joint_map, returned)
+    picked = jnp.take(returned, owner_list, axis=0)
     big_weight_new = apply_update(big_weight, picked[:matrices])
     small_weight_new = apply_update(small_weight, picked[matrices:])
     first_new = first_decay * vec_first + (1.0 - first_decay) * grad_share

time: 136 us -> 138 us (1.015)
  local copies, waits for them, and re-layouts: 17.6 us -> 20.4 us
    unnamed x35 -> x38, local copies, waits for them, and re-layouts: 8.26 us -> 10.5 us
    gather x0 -> x3, local copies, waits for them, and re-layouts: none -> 1.98 us  [the longest x2 1.39 us: per_device(): routed = jnp.take(padded_pieces, owned_index, axis=0).reshape(shards, -1)]
where the time goes in v7:
time: 138 us; the launch traced here: 136 us
  starting transfers between devices  42.3 us (31%)
  waiting for transfers between devices  42 us (30%)
  local copies, waits for them, and re-layouts  20.4 us (15%)
  matrix products  16.4 us (12%)
  other arithmetic  12 us (9%)
  between operations  2.46 us (2%)
    all_to_all x1, waiting for transfers between devices, per_device(): lax.all_to_all(outgoing, 'shard', split_axis=0, concat_axis=0, tiled=True)  20.2 us
    all_to_all x1, starting transfers between devices, per_device(): lax.all_to_all(outgoing, 'shard', split_axis=0, concat_axis=0, tiled=True)  18.4 us
    all_to_all x1, waiting for transfers between devices, per_device(): lax.all_to_all(own_result.reshape(shards, rows_dev, block_width), 'shard'...  17.6 us
    all_to_all x1, starting transfers between devices, per_device(): lax.all_to_all(own_result.reshape(shards, rows_dev, block_width), 'shard'...  10.7 us
    unnamed x38, local copies, waits for them, and re-layouts  10.5 us
    dot_general x4, matrix products, newton_step(): lax.dot_general(full_iterate, polynomial, (((1,), (1,)), ((), ())), prefe...  8.95 us
    dot_general x4, matrix products, gram_block(): lax.dot_general(left_part, right_part, (((0,), (0,)), ((), ())), preferre...  7.41 us
    reduce_sum x2, other arithmetic, normalized(): squares = jnp.sum(values * values)  5.14 us
  transfers between devices with their start and end apart: 6, of which 4 were waited for; matrix products, arithmetic and copies ran while one was open for 8% of the time, Pallas kernels for 0%

profile of v7, /device:TPU:1, one launch (start us, length us, event | category | flops | bytes accessed | tf_op | source)
XLA Modules:
  0.0 135.5 jit_solution(13604481466005715835)
XLA Ops:
  0.6 0.8 slice_bitcast_fusion.2
  1.7 1.0 copy.54
  2.7 1.0 copy.55
  6.8 1.1 reduce.3
  8.1 1.4 %reshape.178 = bf16[128,2,1128]{2,1,0:T(2,128)(2,1)} reshape(bf16[128,2256]{1,0:T(8,128)(2,1)S(1)} %copy.68) | data formatting | bytes 1155072
  9.5 18.4 %all-to-all-start = ((bf16[128,2,1128]{2,1,0:T(2,128)(2,1)}), bf16[128,2,1128]{2,1,0:T(2,128)(2,1)S(1)}, u32[]{:S(2)}, u32[]{:S(2)}) async-start(bf16[128,2,1128]{2,1,0:T(2,128)(2,1)} %reshape.178), calls=%async_computation | async-start | bytes 1179648 | tf_op jit(solution)/shard_map/all_to_all | solution.py:148
  28.6 20.2 %all-to-all-done = bf16[128,2,1128]{2,1,0:T(2,128)(2,1)S(1)} async-done(((bf16[128,2,1128]{2,1,0:T(2,128)(2,1)}), bf16[128,2,1128]{2,1,0:T(2,128)(2,1)S(1)}, u32[]{:S(2)}, u32[]{:S(2)}) %all-to-all-start) | async-done | bytes 577568 | tf_op jit(solution)/shard_map/all_to_all | solution.py:148
  48.8 0.9 reshape.179
  49.7 1.6 %copy.59 = bf16[128,1,2256]{0,2,1:T(8,128)(2,1)S(1)} copy(bf16[128,1,2256]{2,1,0:T(2,128)(2,1)S(1)} %reshape.179) | data formatting | bytes 1155072 | tf_op jit(solution)/shard_map/all_to_all | solution.py:148
  53.7 1.8 %constant_dynamic-update-slice_fusion.4 = (bf16[1280,768]{0,1:T(8,128)(2,1)}, bf16[1280,192]{0,1:T(8,128)(2,1)}) fusion(f32[1,192,1280]{2,1,0:T(8,128)S(1)} %copy-done, f32[1280,192]{0,1:T(8,128)S(1)} %copy.61, pred[]{:T(512)} %get-tuple-element.35), kind=kLoop, calls=%fused_computation.84 | loop fusion | flops 1474559 | bytes 2949121
  55.4 3.1 %collective-permute-start = (bf16[1280,192]{0,1:T(8,128)(2,1)}, bf16[1280,192]{0,1:T(8,128)(2,1)}, u32[]{:S(2)}, u32[]{:S(2)}) collective-permute-start(bf16[1280,192]{0,1:T(8,128)(2,1)} %get-tuple-element.43), channel_id=1, source_target_pairs={{0,1},{1,2},{2,3},{3,0},{4,5},{5,6},{6,7},{7,4},{8,9},{9,10},{10,1... | collective-permute-start | bytes 1474568 | tf_op jit(solution)/shard_map/ppermute | solution.py:101
  58.6 3.4 %collective-permute-start.2 = (bf16[1280,192]{0,1:T(8,128)(2,1)}, bf16[1280,192]{0,1:T(8,128)(2,1)}, u32[]{:S(2)}, u32[]{:S(2)}) collective-permute-start(bf16[1280,192]{0,1:T(8,128)(2,1)} %get-tuple-element.43), channel_id=1, source_target_pairs={{0,3},{1,0},{2,1},{3,2},{4,7},{5,4},{6,5},{7,6},{8,11},{9,8},{10,9... | collective-permute-start | bytes 1474568 | tf_op jit(solution)/shard_map/ppermute | solution.py:102
  61.9 3.5 %fusion.12 = (f32[]{:T(128)}, bf16[192,1280]{1,0:T(8,128)(2,1)S(1)}, f32[1,192,1280]{2,1,0:T(8,128)}, f32[1,192,1280]{2,1,0:T(8,128)}) fusion(f32[1,192,1280]{2,1,0:T(8,128)S(1)} %copy-done.3, f32[1280,192]{0,1:T(8,128)S(1)} %copy.61, pred[]{:T(512)} %get-tuple-element.36, f32[1,192,1280]{2,1,0:T(8,128)S(1)} %copy-done, pred[]{:T(512)} %get-tuple-element.35), kind=kLoop, calls=%fused_computation.30 | loop fusion | flops 3194879 | bytes 5406726 | tf_op jit(solution)/shard_map/reduce_sum | solution.py:56
  67.3 2.3 %collective-permute-done = bf16[1280,192]{0,1:T(8,128)(2,1)} collective-permute-done((bf16[1280,192]{0,1:T(8,128)(2,1)}, bf16[1280,192]{0,1:T(8,128)(2,1)}, u32[]{:S(2)}, u32[]{:S(2)}) %collective-permute-start) | collective-permute-done | bytes 491552 | tf_op jit(solution)/shard_map/ppermute | solution.py:101
  69.6 1.0 slice.47
  70.5 1.9 %collective-permute-start.1 = (bf16[1280,96]{0,1:T(8,128)(2,1)S(1)}, bf16[1280,96]{0,1:T(8,128)(2,1)S(1)}, u32[]{:S(2)}, u32[]{:S(2)}) collective-permute-start(bf16[1280,96]{0,1:T(8,128)(2,1)S(1)} %slice.47), channel_id=1, source_target_pairs={{0,1},{1,2},{2,3},{3,0},{4,5},{5,6},{6,7},{7,4},{8,9},{9,10},{10,1... | collective-permute-start | bytes 737288 | tf_op jit(solution)/shard_map/ppermute | solution.py:104
  72.5 1.2 fusion.4
  73.7 1.0 slice.48
  74.7 4.8 %collective-permute-start.3 = (bf16[1280,96]{0,1:T(8,128)(2,1)S(1)}, bf16[1280,96]{0,1:T(8,128)(2,1)S(1)}, u32[]{:S(2)}, u32[]{:S(2)}) collective-permute-start(bf16[1280,96]{0,1:T(8,128)(2,1)S(1)} %slice.48), channel_id=1, source_target_pairs={{0,3},{1,0},{2,1},{3,2},{4,7},{5,4},{6,5},{7,6},{8,11},{9,8},{10,9... | collective-permute-start | bytes 737288 | tf_op jit(solution)/shard_map/ppermute | solution.py:105
  79.4 1.1 constant_dynamic-update-slice_fusion.3
  80.5 1.8 %collective-permute-done.3 = bf16[1280,96]{0,1:T(8,128)(2,1)S(1)} collective-permute-done((bf16[1280,96]{0,1:T(8,128)(2,1)S(1)}, bf16[1280,96]{0,1:T(8,128)(2,1)S(1)}, u32[]{:S(2)}, u32[]{:S(2)}) %collective-permute-start.3) | collective-permute-done | bytes 245792 | tf_op jit(solution)/shard_map/ppermute | solution.py:105
  82.4 1.1 constant_dynamic-update-slice_fusion
  83.4 1.6 %fusion = f32[]{:T(128)} fusion(bf16[1280,768]{0,1:T(8,128)(2,1)S(1)} %constant_dynamic-update-slice_fusion), kind=kLoop, calls=%fused_computation.4 | loop fusion | flops 2949119 | bytes 1966084 | tf_op jit(solution)/shard_map/reduce_sum | solution.py:56
  85.7 1.8 %convolution_convert_fusion.1 = bf16[768,768]{1,0:T(8,128)(2,1)S(1)} fusion(bf16[1280,768]{0,1:T(8,128)(2,1)S(1)} %constant_dynamic-update-slice_fusion, f32[]{:T(128)S(6)} %add.127), kind=kOutput, calls=%fused_computation.16 | convolution fusion | flops 1513488384 | bytes 3145732 | tf_op jit(solution)/shard_map/dot_general | solution.py:61
  87.5 4.2 %add_convert_fusion = bf16[1280,768]{0,1:T(8,128)(2,1)} fusion(bf16[768,768]{1,0:T(8,128)(2,1)S(1)} %convolution_convert_fusion.1, f32[]{:T(128)S(6)} %add.127, bf16[1280,768]{0,1:T(8,128)(2,1)S(1)} %constant_dynamic-update-slice_fusion), kind=kOutput, calls=%fused_computation.6 | convolution fusion | flops 2428698624 | bytes 5111812 | tf_op jit(solution)/shard_map/dot_general | solution.py:75
  91.7 5.0 %convolution_convert_fusion = bf16[768,768]{1,0:T(8,128)(2,1)} fusion(bf16[1280,768]{0,1:T(8,128)(2,1)} %add_convert_fusion), kind=kOutput, calls=%fused_computation.15 | convolution fusion | flops 1510539264 | bytes 3145728 | tf_op jit(solution)/shard_map/dot_general | solution.py:61
  96.7 3.1 %fusion.5 = bf16[1280,192]{0,1:T(8,128)(2,1)S(1)} fusion(bf16[1280,192]{0,1:T(8,128)(2,1)S(1)} %copy-done.11, bf16[1280,768]{0,1:T(8,128)(2,1)S(1)} %copy-done.12, bf16[768,768]{1,0:T(8,128)(2,1)} %convolution_convert_fusion, pred[]{:T(512)} %get-tuple-element.35), kind=kOutput, calls=%fused_computation.13 | convolution fusion | flops 605945856 | bytes 5210624 | tf_op jit(solution)/shard_map/dot_general | solution.py:75
  100.4 1.6 %reshape.180 = bf16[128,2,960]{2,1,0:T(2,128)(2,1)} reshape(bf16[128,10,192]{2,1,0:T(8,128)(2,1)S(1)} %reshape.158) | data formatting | bytes 983040
  102.0 10.7 %all-to-all-start.1 = ((bf16[128,2,960]{2,1,0:T(2,128)(2,1)}), bf16[128,2,960]{2,1,0:T(2,128)(2,1)S(1)}, u32[]{:S(2)}, u32[]{:S(2)}) async-start(bf16[128,2,960]{2,1,0:T(2,128)(2,1)} %reshape.180), calls=%async_computation.1 | async-start | bytes 1048576 | tf_op jit(solution)/shard_map/all_to_all | solution.py:165
  112.8 1.0 convert_reduce_fusion
  114.5 17.6 %all-to-all-done.1 = bf16[128,2,960]{2,1,0:T(2,128)(2,1)S(1)} async-done(((bf16[128,2,960]{2,1,0:T(2,128)(2,1)}), bf16[128,2,960]{2,1,0:T(2,128)(2,1)S(1)}, u32[]{:S(2)}, u32[]{:S(2)}) %all-to-all-start.1) | async-done | bytes 491552 | tf_op jit(solution)/shard_map/all_to_all | solution.py:165
  132.1 0.8 reshape.181
  (65 shorter events, 11.4 us)
Async XLA Ops:
  4.0 1.4 %copy-start.4 = (f32[1,43008]{1,0:T(1,128)S(1)}, f32[1,43008]{1,0:T(1,128)}, u32[]{:S(2)}) copy-start(f32[1,43008]{1,0:T(1,128)} %param.18) | copy-start | bytes 516100
  7.9 20.1 %copy-start.7 = (s32[2,32]{1,0:T(2,128)S(1)}, s32[2,32]{1,0:T(2,128)}, u32[]{:S(2)}) copy-start(s32[2,32]{1,0:T(2,128)} %param.17) | copy-start | bytes 772
  9.5 39.3 %all-to-all-start = ((bf16[128,2,1128]{2,1,0:T(2,128)(2,1)}), bf16[128,2,1128]{2,1,0:T(2,128)(2,1)S(1)}, u32[]{:S(2)}, u32[]{:S(2)}) async-start(bf16[128,2,1128]{2,1,0:T(2,128)(2,1)} %reshape.178), calls=%async_computation | async-start | bytes 1179648 | tf_op jit(solution)/shard_map/all_to_all | solution.py:148
  51.3 0.8 copy-start.2
  52.4 1.2 copy-start
  53.3 8.6 %copy-start.3 = (f32[1,192,1280]{2,1,0:T(8,128)S(1)}, f32[1,192,1280]{2,1,0:T(8,128)}, u32[]{:S(2)}) copy-start(f32[1,192,1280]{2,1,0:T(8,128)} %param.16) | copy-start | bytes 2949124
  55.4 14.1 %collective-permute-start = (bf16[1280,192]{0,1:T(8,128)(2,1)}, bf16[1280,192]{0,1:T(8,128)(2,1)}, u32[]{:S(2)}, u32[]{:S(2)}) collective-permute-start(bf16[1280,192]{0,1:T(8,128)(2,1)} %get-tuple-element.43), channel_id=1, source_target_pairs={{0,1},{1,2},{2,3},{3,0},{4,5},{5,6},{6,7},{7,4},{8,9},{9,10},{10,1... | collective-permute-start | bytes 1474568 | tf_op jit(solution)/shard_map/ppermute | solution.py:101
  58.6 15.1 %collective-permute-start.2 = (bf16[1280,192]{0,1:T(8,128)(2,1)}, bf16[1280,192]{0,1:T(8,128)(2,1)}, u32[]{:S(2)}, u32[]{:S(2)}) collective-permute-start(bf16[1280,192]{0,1:T(8,128)(2,1)} %get-tuple-element.43), channel_id=1, source_target_pairs={{0,3},{1,0},{2,1},{3,2},{4,7},{5,4},{6,5},{7,6},{8,11},{9,8},{10,9... | collective-permute-start | bytes 1474568 | tf_op jit(solution)/shard_map/ppermute | solution.py:102
  66.9 12.5 %copy-start.1 = (bf16[1280,768]{0,1:T(8,128)(2,1)S(1)}, bf16[1280,768]{0,1:T(8,128)(2,1)}, u32[]{:S(2)}) copy-start(bf16[1280,768]{0,1:T(8,128)(2,1)} %get-tuple-element.42) | copy-start | bytes 5898244
  70.5 10.0 %collective-permute-start.1 = (bf16[1280,96]{0,1:T(8,128)(2,1)S(1)}, bf16[1280,96]{0,1:T(8,128)(2,1)S(1)}, u32[]{:S(2)}, u32[]{:S(2)}) collective-permute-start(bf16[1280,96]{0,1:T(8,128)(2,1)S(1)} %slice.47), channel_id=1, source_target_pairs={{0,1},{1,2},{2,3},{3,0},{4,5},{5,6},{6,7},{7,4},{8,9},{9,10},{10,1... | collective-permute-start | bytes 737288 | tf_op jit(solution)/shard_map/ppermute | solution.py:104
  74.7 7.7 %collective-permute-start.3 = (bf16[1280,96]{0,1:T(8,128)(2,1)S(1)}, bf16[1280,96]{0,1:T(8,128)(2,1)S(1)}, u32[]{:S(2)}, u32[]{:S(2)}) collective-permute-start(bf16[1280,96]{0,1:T(8,128)(2,1)S(1)} %slice.48), channel_id=1, source_target_pairs={{0,3},{1,0},{2,1},{3,2},{4,7},{5,4},{6,5},{7,6},{8,11},{9,8},{10,9... | collective-permute-start | bytes 737288 | tf_op jit(solution)/shard_map/ppermute | solution.py:105
  91.7 5.0 %copy-start.11 = (bf16[1280,192]{0,1:T(8,128)(2,1)S(1)}, bf16[1280,192]{0,1:T(8,128)(2,1)}, u32[]{:S(2)}) copy-start(bf16[1280,192]{0,1:T(8,128)(2,1)} %fusion.4) | copy-start | bytes 1474564
  91.7 5.0 %copy-start.12 = (bf16[1280,768]{0,1:T(8,128)(2,1)S(1)}, bf16[1280,768]{0,1:T(8,128)(2,1)}, u32[]{:S(2)}) copy-start(bf16[1280,768]{0,1:T(8,128)(2,1)} %add_convert_fusion) | copy-start | bytes 5898244
  100.1 13.8 %copy-start.8 = (f32[336]{0:T(512)S(1)}, f32[336]{0:T(512)}, u32[]{:S(2)}) copy-start(f32[336]{0:T(512)} %param.19) | copy-start | bytes 4036
  100.1 13.8 %copy-start.9 = (f32[336]{0:T(512)S(1)}, f32[336]{0:T(512)}, u32[]{:S(2)}) copy-start(f32[336]{0:T(512)} %param.20) | copy-start | bytes 4036
  100.1 13.8 %copy-start.10 = (f32[336]{0:T(512)S(1)}, f32[336]{0:T(512)}, u32[]{:S(2)}) copy-start(f32[336]{0:T(512)} %param.21) | copy-start | bytes 4036
  102.0 30.1 %all-to-all-start.1 = ((bf16[128,2,960]{2,1,0:T(2,128)(2,1)}), bf16[128,2,960]{2,1,0:T(2,128)(2,1)S(1)}, u32[]{:S(2)}, u32[]{:S(2)}) async-start(bf16[128,2,960]{2,1,0:T(2,128)(2,1)} %reshape.180), calls=%async_computation.1 | async-start | bytes 1048576 | tf_op jit(solution)/shard_map/all_to_all | solution.py:165
  112.7 21.0 %copy-start.5 = (bf16[32,10,192]{2,0,1:T(8,128)(2,1)S(1)}, bf16[32,10,192]{2,0,1:T(8,128)(2,1)}, u32[]{:S(2)}) copy-start(bf16[32,10,192]{2,0,1:T(8,128)(2,1)} %param.15) | copy-start | bytes 368644
  112.7 20.9 %copy-start.6 = (bf16[32,10,192]{2,0,1:T(8,128)(2,1)S(1)}, bf16[32,10,192]{2,0,1:T(8,128)(2,1)}, u32[]{:S(2)}) copy-start(bf16[32,10,192]{2,0,1:T(8,128)(2,1)} %param.12) | copy-start | bytes 368644
